TPU v7x, 512 devices: a whole 4x4x16 slice. The times are simulated.
512 devices in a mesh: tm: 32 (over z, core), tile: 16 (over y, x).
Axes of the slice: x: 4, y: 4, z: 16, core: 2. Of those that a mesh axis runs over, the one named last changes fastest.
Arguments:
- tile_rows: int32 [32, 1024], P('tm', 'tile'), may hold values from 0 to 31
- tile_cols: int32 [32, 1024], P('tm', 'tile'), may hold values from 0 to 7
- live_tiles: int32 [32, 16], P('tm', 'tile'), may hold values from 32 to 64, as said below
- factor_tiles: bfloat16 [32, 1024, 128, 128], P('tm', 'tile'), may hold values from -0.09375 to 0.09375
- bus_inverse: bfloat16 [32, 128, 128, 128], P('tm', 'tile'), may hold values from -0.5 to 0.5
- bus_coupling: bfloat16 [32, 128, 128, 128], P('tm', 'tile'), may hold values from -0.5 to 0.5
- bus_rhs: bfloat16 [32, 128, 64, 128], P('tm', 'tile'), may hold values from -6 to 6
- row_inverse: bfloat16 [32, 32, 128, 128], P('tm', 'tile'), may hold values from -0.5 to 0.5
- row_rhs: bfloat16 [32, 32, 64, 128], P('tm', 'tile'), may hold values from -6 to 6
- coupling_inverse: float32 [32, 128, 128], P('tm')
- coupling_next: float32 [32, 128, 128], P('tm')
- coupling_rhs: float32 [32, 64, 128], P('tm'), may hold values from -6 to 6
Outputs:
- multipliers: float32 [32, 64, 128], P('tm')
- bus_values: bfloat16 [32, 128, 64, 128], P('tm', 'tile')
- row_values: float32 [32, 32, 64, 128], P('tm', 'tile')
Inputs may be any that keep to these rules, and one draw needn't show every extreme that they name: `live_tiles`: at least one device uses all 64 of its slots.
All inputs are finite; a program needn't handle non-finite values.
Results may differ from a plain program's by a relative error of at most 0.006.
Values sent between devices are 32-bit elements; how exact they have to be, the bound alone decides.
No kernel may reach another device: no remote copies, remote signals or barrier semaphores. Data moves between devices by JAX's collectives and lax.ppermute only.
A program may use at most 64 MiB of HBM per device.

v0:
```python
import jax
import jax.numpy as jnp
from jax import lax
from jax.sharding import PartitionSpec as P

HIGH = lax.Precision.HIGHEST


def passed_along(x, axis, by):
    size = lax.axis_size(axis)
    pairs = [(i, i + by) for i in range(size) if 0 <= i + by < size]
    return lax.ppermute(x, axis, pairs)


def per_device(
    tile_rows,
    tile_cols,
    live_tiles,
    factor_tiles,
    bus_inverse,
    bus_coupling,
    bus_rhs,
    row_inverse,
    row_rhs,
    coupling_inverse,
    coupling_next,
    coupling_rhs,
):
    inverse = coupling_inverse[0]
    nextmat = coupling_next[0]
    rhside = coupling_rhs[0]
    start_zero = jnp.zeros(rhside.shape, jnp.float32)

    def sweep(sweep_index, current):
        beyond = passed_along(current, "tm", -1)
        return jnp.dot(rhside - jnp.dot(beyond, nextmat, precision=HIGH), inverse, precision=HIGH)

    multipliers = lax.fori_loop(0, lax.axis_size("tm"), sweep, start_zero)
    rounded = multipliers.astype(jnp.bfloat16)
    coupled = jnp.einsum(
        "rb,jbc->jrc", rounded, bus_coupling[0], preferred_element_type=jnp.float32
    )
    bus_work = (bus_rhs[0].astype(jnp.float32) - coupled).astype(jnp.bfloat16)
    bus_values = jnp.einsum(
        "jrb,jbc->jrc", bus_work, bus_inverse[0], preferred_element_type=jnp.float32
    ).astype(jnp.bfloat16)
    rows = tile_rows[0]
    cols = tile_cols[0]
    slots = rows.shape[0]
    buses_here = bus_values.shape[0]
    select_table = (cols[:, None] == jnp.arange(buses_here)[None, :]).astype(jnp.bfloat16)
    chosen = jnp.einsum(
        "kj,jrb->krb", select_table, bus_values, preferred_element_type=jnp.float32
    ).astype(jnp.bfloat16)
    live_mask = (jnp.arange(slots) < live_tiles[0, 0]).astype(jnp.float32)
    products = jnp.einsum(
        "krb,kbc->krc", chosen, factor_tiles[0], preferred_element_type=jnp.float32
    )
    products = products * live_mask[:, None, None]
    owned = row_rhs.shape[1]
    total_rows = owned * lax.axis_size("tile")
    onehot = (rows[:, None] == jnp.arange(total_rows)[None, :]).astype(jnp.float32)
    whole = jnp.einsum("ki,krc->irc", onehot, products, precision=HIGH)
    summed = lax.psum(whole, "tile")
    partials = lax.dynamic_slice_in_dim(summed, lax.axis_index("tile") * owned, owned, 0)
    row_work = (row_rhs[0].astype(jnp.float32) - partials).astype(jnp.bfloat16)
    row_values = jnp.einsum(
        "irb,ibc->irc", row_work, row_inverse[0], preferred_element_type=jnp.float32
    )
    return (multipliers[None], bus_values[None], row_values[None])


def solution(mesh):
    placed = (
        P("tm", "tile"),
        P("tm", "tile"),
        P("tm", "tile"),
        P("tm", "tile", None, None),
        P("tm", "tile", None, None),
        P("tm", "tile", None, None),
        P("tm", "tile", None, None),
        P("tm", "tile", None, None),
        P("tm", "tile", None, None),
        P("tm", None, None),
        P("tm", None, None),
        P("tm", None, None),
    )
    return jax.shard_map(
        per_device,
        mesh=mesh,
        in_specs=placed,
        out_specs=(P("tm", None, None), P("tm", "tile", None, None), P("tm", "tile", None, None)),
        check_vma=False,
    )
```

profile of v0, /device:TPU:6, one launch (start us, length us, event | category | flops | bytes accessed | tf_op | source)
XLA Modules:
  0.0 416.5 jit_solution(4158306744137098736)
XLA Ops:
  8.0 255.0 %while.10 = (s32[]{:T(128)}, f32[64,128]{1,0:T(8,128)S(1)}, f32[128,128]{1,0:T(8,128)}, f32[64,128]{1,0:T(8,128)}, f32[128,128]{1,0:T(8,128)}, /*index=5*/s32[]{:T(128)}) while((s32[]{:T(128)}, f32[64,128]{1,0:T(8,128)S(1)}, f32[128,128]{1,0:T(8,128)}, f32[64,128]{1,0:T(8,128)}, f32[128,128]{1,0:T(8,128)}, /*index=5*/s32[]{:T(128)}) %tuple.29), condition=%wide.region_1.0_spmd, body=%wide.region_0.0_spmd.sunk | while | flops 25174016 | bytes 426093 | solution.py:38
  21.7 3.9 collective-permute-done
  29.0 3.9 collective-permute-done
  36.3 3.9 collective-permute-done
  43.6 3.9 collective-permute-done
  50.9 3.9 collective-permute-done
  58.2 3.9 collective-permute-done
  65.5 3.9 collective-permute-done
  72.9 3.9 collective-permute-done
  80.2 3.9 collective-permute-done
  87.5 3.9 collective-permute-done
  94.8 4.2 %collective-permute-done = f32[64,128]{1,0:T(8,128)S(1)} collective-permute-done((f32[64,128]{1,0:T(8,128)S(1)}, f32[64,128]{1,0:T(8,128)S(1)}, u32[]{:S(2)}, u32[]{:S(2)}) %collective-permute-start) | collective-permute-done | bytes 32800 | tf_op jit(solution)/shard_map/while/body/eval_jaxpr/ppermute | solution.py:12
  102.4 5.1 %collective-permute-done = f32[64,128]{1,0:T(8,128)S(1)} collective-permute-done((f32[64,128]{1,0:T(8,128)S(1)}, f32[64,128]{1,0:T(8,128)S(1)}, u32[]{:S(2)}, u32[]{:S(2)}) %collective-permute-start) | collective-permute-done | bytes 32800 | tf_op jit(solution)/shard_map/while/body/eval_jaxpr/ppermute | solution.py:12
  110.9 5.1 %collective-permute-done = f32[64,128]{1,0:T(8,128)S(1)} collective-permute-done((f32[64,128]{1,0:T(8,128)S(1)}, f32[64,128]{1,0:T(8,128)S(1)}, u32[]{:S(2)}, u32[]{:S(2)}) %collective-permute-start) | collective-permute-done | bytes 32800 | tf_op jit(solution)/shard_map/while/body/eval_jaxpr/ppermute | solution.py:12
  119.4 5.1 %collective-permute-done = f32[64,128]{1,0:T(8,128)S(1)} collective-permute-done((f32[64,128]{1,0:T(8,128)S(1)}, f32[64,128]{1,0:T(8,128)S(1)}, u32[]{:S(2)}, u32[]{:S(2)}) %collective-permute-start) | collective-permute-done | bytes 32800 | tf_op jit(solution)/shard_map/while/body/eval_jaxpr/ppermute | solution.py:12
  128.0 5.1 %collective-permute-done = f32[64,128]{1,0:T(8,128)S(1)} collective-permute-done((f32[64,128]{1,0:T(8,128)S(1)}, f32[64,128]{1,0:T(8,128)S(1)}, u32[]{:S(2)}, u32[]{:S(2)}) %collective-permute-start) | collective-permute-done | bytes 32800 | tf_op jit(solution)/shard_map/while/body/eval_jaxpr/ppermute | solution.py:12
  136.5 5.1 %collective-permute-done = f32[64,128]{1,0:T(8,128)S(1)} collective-permute-done((f32[64,128]{1,0:T(8,128)S(1)}, f32[64,128]{1,0:T(8,128)S(1)}, u32[]{:S(2)}, u32[]{:S(2)}) %collective-permute-start) | collective-permute-done | bytes 32800 | tf_op jit(solution)/shard_map/while/body/eval_jaxpr/ppermute | solution.py:12
  145.0 5.1 %collective-permute-done = f32[64,128]{1,0:T(8,128)S(1)} collective-permute-done((f32[64,128]{1,0:T(8,128)S(1)}, f32[64,128]{1,0:T(8,128)S(1)}, u32[]{:S(2)}, u32[]{:S(2)}) %collective-permute-start) | collective-permute-done | bytes 32800 | tf_op jit(solution)/shard_map/while/body/eval_jaxpr/ppermute | solution.py:12
  153.5 5.1 %collective-permute-done = f32[64,128]{1,0:T(8,128)S(1)} collective-permute-done((f32[64,128]{1,0:T(8,128)S(1)}, f32[64,128]{1,0:T(8,128)S(1)}, u32[]{:S(2)}, u32[]{:S(2)}) %collective-permute-start) | collective-permute-done | bytes 32800 | tf_op jit(solution)/shard_map/while/body/eval_jaxpr/ppermute | solution.py:12
  162.1 5.1 %collective-permute-done = f32[64,128]{1,0:T(8,128)S(1)} collective-permute-done((f32[64,128]{1,0:T(8,128)S(1)}, f32[64,128]{1,0:T(8,128)S(1)}, u32[]{:S(2)}, u32[]{:S(2)}) %collective-permute-start) | collective-permute-done | bytes 32800 | tf_op jit(solution)/shard_map/while/body/eval_jaxpr/ppermute | solution.py:12
  170.6 5.1 %collective-permute-done = f32[64,128]{1,0:T(8,128)S(1)} collective-permute-done((f32[64,128]{1,0:T(8,128)S(1)}, f32[64,128]{1,0:T(8,128)S(1)}, u32[]{:S(2)}, u32[]{:S(2)}) %collective-permute-start) | collective-permute-done | bytes 32800 | tf_op jit(solution)/shard_map/while/body/eval_jaxpr/ppermute | solution.py:12
  179.1 5.1 %collective-permute-done = f32[64,128]{1,0:T(8,128)S(1)} collective-permute-done((f32[64,128]{1,0:T(8,128)S(1)}, f32[64,128]{1,0:T(8,128)S(1)}, u32[]{:S(2)}, u32[]{:S(2)}) %collective-permute-start) | collective-permute-done | bytes 32800 | tf_op jit(solution)/shard_map/while/body/eval_jaxpr/ppermute | solution.py:12
  187.6 5.1 %collective-permute-done = f32[64,128]{1,0:T(8,128)S(1)} collective-permute-done((f32[64,128]{1,0:T(8,128)S(1)}, f32[64,128]{1,0:T(8,128)S(1)}, u32[]{:S(2)}, u32[]{:S(2)}) %collective-permute-start) | collective-permute-done | bytes 32800 | tf_op jit(solution)/shard_map/while/body/eval_jaxpr/ppermute | solution.py:12
  196.1 5.1 %collective-permute-done = f32[64,128]{1,0:T(8,128)S(1)} collective-permute-done((f32[64,128]{1,0:T(8,128)S(1)}, f32[64,128]{1,0:T(8,128)S(1)}, u32[]{:S(2)}, u32[]{:S(2)}) %collective-permute-start) | collective-permute-done | bytes 32800 | tf_op jit(solution)/shard_map/while/body/eval_jaxpr/ppermute | solution.py:12
  204.7 5.1 %collective-permute-done = f32[64,128]{1,0:T(8,128)S(1)} collective-permute-done((f32[64,128]{1,0:T(8,128)S(1)}, f32[64,128]{1,0:T(8,128)S(1)}, u32[]{:S(2)}, u32[]{:S(2)}) %collective-permute-start) | collective-permute-done | bytes 32800 | tf_op jit(solution)/shard_map/while/body/eval_jaxpr/ppermute | solution.py:12
  213.2 5.1 %collective-permute-done = f32[64,128]{1,0:T(8,128)S(1)} collective-permute-done((f32[64,128]{1,0:T(8,128)S(1)}, f32[64,128]{1,0:T(8,128)S(1)}, u32[]{:S(2)}, u32[]{:S(2)}) %collective-permute-start) | collective-permute-done | bytes 32800 | tf_op jit(solution)/shard_map/while/body/eval_jaxpr/ppermute | solution.py:12
  221.7 5.1 %collective-permute-done = f32[64,128]{1,0:T(8,128)S(1)} collective-permute-done((f32[64,128]{1,0:T(8,128)S(1)}, f32[64,128]{1,0:T(8,128)S(1)}, u32[]{:S(2)}, u32[]{:S(2)}) %collective-permute-start) | collective-permute-done | bytes 32800 | tf_op jit(solution)/shard_map/while/body/eval_jaxpr/ppermute | solution.py:12
  230.2 5.1 %collective-permute-done = f32[64,128]{1,0:T(8,128)S(1)} collective-permute-done((f32[64,128]{1,0:T(8,128)S(1)}, f32[64,128]{1,0:T(8,128)S(1)}, u32[]{:S(2)}, u32[]{:S(2)}) %collective-permute-start) | collective-permute-done | bytes 32800 | tf_op jit(solution)/shard_map/while/body/eval_jaxpr/ppermute | solution.py:12
  238.8 5.1 %collective-permute-done = f32[64,128]{1,0:T(8,128)S(1)} collective-permute-done((f32[64,128]{1,0:T(8,128)S(1)}, f32[64,128]{1,0:T(8,128)S(1)}, u32[]{:S(2)}, u32[]{:S(2)}) %collective-permute-start) | collective-permute-done | bytes 32800 | tf_op jit(solution)/shard_map/while/body/eval_jaxpr/ppermute | solution.py:12
  247.3 5.1 %collective-permute-done = f32[64,128]{1,0:T(8,128)S(1)} collective-permute-done((f32[64,128]{1,0:T(8,128)S(1)}, f32[64,128]{1,0:T(8,128)S(1)}, u32[]{:S(2)}, u32[]{:S(2)}) %collective-permute-start) | collective-permute-done | bytes 32800 | tf_op jit(solution)/shard_map/while/body/eval_jaxpr/ppermute | solution.py:12
  255.8 5.1 %collective-permute-done = f32[64,128]{1,0:T(8,128)S(1)} collective-permute-done((f32[64,128]{1,0:T(8,128)S(1)}, f32[64,128]{1,0:T(8,128)S(1)}, u32[]{:S(2)}, u32[]{:S(2)}) %collective-permute-start) | collective-permute-done | bytes 32800 | tf_op jit(solution)/shard_map/while/body/eval_jaxpr/ppermute | solution.py:12
  270.0 138.0 %all-reduce.2.cloned.1.call-done = f32[32,64,128]{2,1,0:T(8,128)} async-done(((f32[32,64,128]{2,1,0:T(8,128)}), f32[32,64,128]{2,1,0:T(8,128)}) %all-reduce.2.cloned.1.call-update) | async-done | bytes 1048592 | tf_op jit(solution)/shard_map/psum | solution.py:64
  (122 shorter events, 121.0 us)
Async XLA Ops:
  7.2 400.9 %all-reduce.2.cloned.1.call-start = ((), (), s32[]{:S(2)}) async-start(), calls=%async_computation | async-start | bytes 2097152 | tf_op jit(solution)/shard_map/psum | solution.py:64
  13.2 5.0 %collective-permute-start = (f32[64,128]{1,0:T(8,128)S(1)}, f32[64,128]{1,0:T(8,128)S(1)}, u32[]{:S(2)}, u32[]{:S(2)}) collective-permute-start(f32[64,128]{1,0:T(8,128)S(1)} %get-tuple-element.79), channel_id=1, source_target_pairs={{16,0},{32,16},{48,32},{64,48},{80,64},{96,80},{112,96},{128,112},... | collective-permute-start | bytes 98312 | tf_op jit(solution)/shard_map/while/body/eval_jaxpr/ppermute | solution.py:12
  20.4 5.2 %collective-permute-start = (f32[64,128]{1,0:T(8,128)S(1)}, f32[64,128]{1,0:T(8,128)S(1)}, u32[]{:S(2)}, u32[]{:S(2)}) collective-permute-start(f32[64,128]{1,0:T(8,128)S(1)} %get-tuple-element.79), channel_id=1, source_target_pairs={{16,0},{32,16},{48,32},{64,48},{80,64},{96,80},{112,96},{128,112},... | collective-permute-start | bytes 98312 | tf_op jit(solution)/shard_map/while/body/eval_jaxpr/ppermute | solution.py:12
  27.7 5.2 %collective-permute-start = (f32[64,128]{1,0:T(8,128)S(1)}, f32[64,128]{1,0:T(8,128)S(1)}, u32[]{:S(2)}, u32[]{:S(2)}) collective-permute-start(f32[64,128]{1,0:T(8,128)S(1)} %get-tuple-element.79), channel_id=1, source_target_pairs={{16,0},{32,16},{48,32},{64,48},{80,64},{96,80},{112,96},{128,112},... | collective-permute-start | bytes 98312 | tf_op jit(solution)/shard_map/while/body/eval_jaxpr/ppermute | solution.py:12
  35.0 5.2 %collective-permute-start = (f32[64,128]{1,0:T(8,128)S(1)}, f32[64,128]{1,0:T(8,128)S(1)}, u32[]{:S(2)}, u32[]{:S(2)}) collective-permute-start(f32[64,128]{1,0:T(8,128)S(1)} %get-tuple-element.79), channel_id=1, source_target_pairs={{16,0},{32,16},{48,32},{64,48},{80,64},{96,80},{112,96},{128,112},... | collective-permute-start | bytes 98312 | tf_op jit(solution)/shard_map/while/body/eval_jaxpr/ppermute | solution.py:12
  42.3 5.2 %collective-permute-start = (f32[64,128]{1,0:T(8,128)S(1)}, f32[64,128]{1,0:T(8,128)S(1)}, u32[]{:S(2)}, u32[]{:S(2)}) collective-permute-start(f32[64,128]{1,0:T(8,128)S(1)} %get-tuple-element.79), channel_id=1, source_target_pairs={{16,0},{32,16},{48,32},{64,48},{80,64},{96,80},{112,96},{128,112},... | collective-permute-start | bytes 98312 | tf_op jit(solution)/shard_map/while/body/eval_jaxpr/ppermute | solution.py:12
  49.6 5.2 %collective-permute-start = (f32[64,128]{1,0:T(8,128)S(1)}, f32[64,128]{1,0:T(8,128)S(1)}, u32[]{:S(2)}, u32[]{:S(2)}) collective-permute-start(f32[64,128]{1,0:T(8,128)S(1)} %get-tuple-element.79), channel_id=1, source_target_pairs={{16,0},{32,16},{48,32},{64,48},{80,64},{96,80},{112,96},{128,112},... | collective-permute-start | bytes 98312 | tf_op jit(solution)/shard_map/while/body/eval_jaxpr/ppermute | solution.py:12
  56.9 5.2 %collective-permute-start = (f32[64,128]{1,0:T(8,128)S(1)}, f32[64,128]{1,0:T(8,128)S(1)}, u32[]{:S(2)}, u32[]{:S(2)}) collective-permute-start(f32[64,128]{1,0:T(8,128)S(1)} %get-tuple-element.79), channel_id=1, source_target_pairs={{16,0},{32,16},{48,32},{64,48},{80,64},{96,80},{112,96},{128,112},... | collective-permute-start | bytes 98312 | tf_op jit(solution)/shard_map/while/body/eval_jaxpr/ppermute | solution.py:12
  64.2 5.2 %collective-permute-start = (f32[64,128]{1,0:T(8,128)S(1)}, f32[64,128]{1,0:T(8,128)S(1)}, u32[]{:S(2)}, u32[]{:S(2)}) collective-permute-start(f32[64,128]{1,0:T(8,128)S(1)} %get-tuple-element.79), channel_id=1, source_target_pairs={{16,0},{32,16},{48,32},{64,48},{80,64},{96,80},{112,96},{128,112},... | collective-permute-start | bytes 98312 | tf_op jit(solution)/shard_map/while/body/eval_jaxpr/ppermute | solution.py:12
  71.6 5.2 %collective-permute-start = (f32[64,128]{1,0:T(8,128)S(1)}, f32[64,128]{1,0:T(8,128)S(1)}, u32[]{:S(2)}, u32[]{:S(2)}) collective-permute-start(f32[64,128]{1,0:T(8,128)S(1)} %get-tuple-element.79), channel_id=1, source_target_pairs={{16,0},{32,16},{48,32},{64,48},{80,64},{96,80},{112,96},{128,112},... | collective-permute-start | bytes 98312 | tf_op jit(solution)/shard_map/while/body/eval_jaxpr/ppermute | solution.py:12
  78.9 5.2 %collective-permute-start = (f32[64,128]{1,0:T(8,128)S(1)}, f32[64,128]{1,0:T(8,128)S(1)}, u32[]{:S(2)}, u32[]{:S(2)}) collective-permute-start(f32[64,128]{1,0:T(8,128)S(1)} %get-tuple-element.79), channel_id=1, source_target_pairs={{16,0},{32,16},{48,32},{64,48},{80,64},{96,80},{112,96},{128,112},... | collective-permute-start | bytes 98312 | tf_op jit(solution)/shard_map/while/body/eval_jaxpr/ppermute | solution.py:12
  86.2 5.2 %collective-permute-start = (f32[64,128]{1,0:T(8,128)S(1)}, f32[64,128]{1,0:T(8,128)S(1)}, u32[]{:S(2)}, u32[]{:S(2)}) collective-permute-start(f32[64,128]{1,0:T(8,128)S(1)} %get-tuple-element.79), channel_id=1, source_target_pairs={{16,0},{32,16},{48,32},{64,48},{80,64},{96,80},{112,96},{128,112},... | collective-permute-start | bytes 98312 | tf_op jit(solution)/shard_map/while/body/eval_jaxpr/ppermute | solution.py:12
  93.5 5.5 %collective-permute-start = (f32[64,128]{1,0:T(8,128)S(1)}, f32[64,128]{1,0:T(8,128)S(1)}, u32[]{:S(2)}, u32[]{:S(2)}) collective-permute-start(f32[64,128]{1,0:T(8,128)S(1)} %get-tuple-element.79), channel_id=1, source_target_pairs={{16,0},{32,16},{48,32},{64,48},{80,64},{96,80},{112,96},{128,112},... | collective-permute-start | bytes 98312 | tf_op jit(solution)/shard_map/while/body/eval_jaxpr/ppermute | solution.py:12
  101.1 6.4 %collective-permute-start = (f32[64,128]{1,0:T(8,128)S(1)}, f32[64,128]{1,0:T(8,128)S(1)}, u32[]{:S(2)}, u32[]{:S(2)}) collective-permute-start(f32[64,128]{1,0:T(8,128)S(1)} %get-tuple-element.79), channel_id=1, source_target_pairs={{16,0},{32,16},{48,32},{64,48},{80,64},{96,80},{112,96},{128,112},... | collective-permute-start | bytes 98312 | tf_op jit(solution)/shard_map/while/body/eval_jaxpr/ppermute | solution.py:12
  109.6 6.4 %collective-permute-start = (f32[64,128]{1,0:T(8,128)S(1)}, f32[64,128]{1,0:T(8,128)S(1)}, u32[]{:S(2)}, u32[]{:S(2)}) collective-permute-start(f32[64,128]{1,0:T(8,128)S(1)} %get-tuple-element.79), channel_id=1, source_target_pairs={{16,0},{32,16},{48,32},{64,48},{80,64},{96,80},{112,96},{128,112},... | collective-permute-start | bytes 98312 | tf_op jit(solution)/shard_map/while/body/eval_jaxpr/ppermute | solution.py:12
  118.1 6.4 %collective-permute-start = (f32[64,128]{1,0:T(8,128)S(1)}, f32[64,128]{1,0:T(8,128)S(1)}, u32[]{:S(2)}, u32[]{:S(2)}) collective-permute-start(f32[64,128]{1,0:T(8,128)S(1)} %get-tuple-element.79), channel_id=1, source_target_pairs={{16,0},{32,16},{48,32},{64,48},{80,64},{96,80},{112,96},{128,112},... | collective-permute-start | bytes 98312 | tf_op jit(solution)/shard_map/while/body/eval_jaxpr/ppermute | solution.py:12
  126.7 6.4 %collective-permute-start = (f32[64,128]{1,0:T(8,128)S(1)}, f32[64,128]{1,0:T(8,128)S(1)}, u32[]{:S(2)}, u32[]{:S(2)}) collective-permute-start(f32[64,128]{1,0:T(8,128)S(1)} %get-tuple-element.79), channel_id=1, source_target_pairs={{16,0},{32,16},{48,32},{64,48},{80,64},{96,80},{112,96},{128,112},... | collective-permute-start | bytes 98312 | tf_op jit(solution)/shard_map/while/body/eval_jaxpr/ppermute | solution.py:12
  135.2 6.4 %collective-permute-start = (f32[64,128]{1,0:T(8,128)S(1)}, f32[64,128]{1,0:T(8,128)S(1)}, u32[]{:S(2)}, u32[]{:S(2)}) collective-permute-start(f32[64,128]{1,0:T(8,128)S(1)} %get-tuple-element.79), channel_id=1, source_target_pairs={{16,0},{32,16},{48,32},{64,48},{80,64},{96,80},{112,96},{128,112},... | collective-permute-start | bytes 98312 | tf_op jit(solution)/shard_map/while/body/eval_jaxpr/ppermute | solution.py:12
  143.7 6.4 %collective-permute-start = (f32[64,128]{1,0:T(8,128)S(1)}, f32[64,128]{1,0:T(8,128)S(1)}, u32[]{:S(2)}, u32[]{:S(2)}) collective-permute-start(f32[64,128]{1,0:T(8,128)S(1)} %get-tuple-element.79), channel_id=1, source_target_pairs={{16,0},{32,16},{48,32},{64,48},{80,64},{96,80},{112,96},{128,112},... | collective-permute-start | bytes 98312 | tf_op jit(solution)/shard_map/while/body/eval_jaxpr/ppermute | solution.py:12
  152.2 6.4 %collective-permute-start = (f32[64,128]{1,0:T(8,128)S(1)}, f32[64,128]{1,0:T(8,128)S(1)}, u32[]{:S(2)}, u32[]{:S(2)}) collective-permute-start(f32[64,128]{1,0:T(8,128)S(1)} %get-tuple-element.79), channel_id=1, source_target_pairs={{16,0},{32,16},{48,32},{64,48},{80,64},{96,80},{112,96},{128,112},... | collective-permute-start | bytes 98312 | tf_op jit(solution)/shard_map/while/body/eval_jaxpr/ppermute | solution.py:12
  160.8 6.4 %collective-permute-start = (f32[64,128]{1,0:T(8,128)S(1)}, f32[64,128]{1,0:T(8,128)S(1)}, u32[]{:S(2)}, u32[]{:S(2)}) collective-permute-start(f32[64,128]{1,0:T(8,128)S(1)} %get-tuple-element.79), channel_id=1, source_target_pairs={{16,0},{32,16},{48,32},{64,48},{80,64},{96,80},{112,96},{128,112},... | collective-permute-start | bytes 98312 | tf_op jit(solution)/shard_map/while/body/eval_jaxpr/ppermute | solution.py:12
  169.3 6.4 %collective-permute-start = (f32[64,128]{1,0:T(8,128)S(1)}, f32[64,128]{1,0:T(8,128)S(1)}, u32[]{:S(2)}, u32[]{:S(2)}) collective-permute-start(f32[64,128]{1,0:T(8,128)S(1)} %get-tuple-element.79), channel_id=1, source_target_pairs={{16,0},{32,16},{48,32},{64,48},{80,64},{96,80},{112,96},{128,112},... | collective-permute-start | bytes 98312 | tf_op jit(solution)/shard_map/while/body/eval_jaxpr/ppermute | solution.py:12
  177.8 6.4 %collective-permute-start = (f32[64,128]{1,0:T(8,128)S(1)}, f32[64,128]{1,0:T(8,128)S(1)}, u32[]{:S(2)}, u32[]{:S(2)}) collective-permute-start(f32[64,128]{1,0:T(8,128)S(1)} %get-tuple-element.79), channel_id=1, source_target_pairs={{16,0},{32,16},{48,32},{64,48},{80,64},{96,80},{112,96},{128,112},... | collective-permute-start | bytes 98312 | tf_op jit(solution)/shard_map/while/body/eval_jaxpr/ppermute | solution.py:12
  186.3 6.4 %collective-permute-start = (f32[64,128]{1,0:T(8,128)S(1)}, f32[64,128]{1,0:T(8,128)S(1)}, u32[]{:S(2)}, u32[]{:S(2)}) collective-permute-start(f32[64,128]{1,0:T(8,128)S(1)} %get-tuple-element.79), channel_id=1, source_target_pairs={{16,0},{32,16},{48,32},{64,48},{80,64},{96,80},{112,96},{128,112},... | collective-permute-start | bytes 98312 | tf_op jit(solution)/shard_map/while/body/eval_jaxpr/ppermute | solution.py:12
  194.8 6.4 %collective-permute-start = (f32[64,128]{1,0:T(8,128)S(1)}, f32[64,128]{1,0:T(8,128)S(1)}, u32[]{:S(2)}, u32[]{:S(2)}) collective-permute-start(f32[64,128]{1,0:T(8,128)S(1)} %get-tuple-element.79), channel_id=1, source_target_pairs={{16,0},{32,16},{48,32},{64,48},{80,64},{96,80},{112,96},{128,112},... | collective-permute-start | bytes 98312 | tf_op jit(solution)/shard_map/while/body/eval_jaxpr/ppermute | solution.py:12
  203.4 6.4 %collective-permute-start = (f32[64,128]{1,0:T(8,128)S(1)}, f32[64,128]{1,0:T(8,128)S(1)}, u32[]{:S(2)}, u32[]{:S(2)}) collective-permute-start(f32[64,128]{1,0:T(8,128)S(1)} %get-tuple-element.79), channel_id=1, source_target_pairs={{16,0},{32,16},{48,32},{64,48},{80,64},{96,80},{112,96},{128,112},... | collective-permute-start | bytes 98312 | tf_op jit(solution)/shard_map/while/body/eval_jaxpr/ppermute | solution.py:12
  211.9 6.4 %collective-permute-start = (f32[64,128]{1,0:T(8,128)S(1)}, f32[64,128]{1,0:T(8,128)S(1)}, u32[]{:S(2)}, u32[]{:S(2)}) collective-permute-start(f32[64,128]{1,0:T(8,128)S(1)} %get-tuple-element.79), channel_id=1, source_target_pairs={{16,0},{32,16},{48,32},{64,48},{80,64},{96,80},{112,96},{128,112},... | collective-permute-start | bytes 98312 | tf_op jit(solution)/shard_map/while/body/eval_jaxpr/ppermute | solution.py:12
  220.4 6.4 %collective-permute-start = (f32[64,128]{1,0:T(8,128)S(1)}, f32[64,128]{1,0:T(8,128)S(1)}, u32[]{:S(2)}, u32[]{:S(2)}) collective-permute-start(f32[64,128]{1,0:T(8,128)S(1)} %get-tuple-element.79), channel_id=1, source_target_pairs={{16,0},{32,16},{48,32},{64,48},{80,64},{96,80},{112,96},{128,112},... | collective-permute-start | bytes 98312 | tf_op jit(solution)/shard_map/while/body/eval_jaxpr/ppermute | solution.py:12
  228.9 6.4 %collective-permute-start = (f32[64,128]{1,0:T(8,128)S(1)}, f32[64,128]{1,0:T(8,128)S(1)}, u32[]{:S(2)}, u32[]{:S(2)}) collective-permute-start(f32[64,128]{1,0:T(8,128)S(1)} %get-tuple-element.79), channel_id=1, source_target_pairs={{16,0},{32,16},{48,32},{64,48},{80,64},{96,80},{112,96},{128,112},... | collective-permute-start | bytes 98312 | tf_op jit(solution)/shard_map/while/body/eval_jaxpr/ppermute | solution.py:12
  237.5 6.4 %collective-permute-start = (f32[64,128]{1,0:T(8,128)S(1)}, f32[64,128]{1,0:T(8,128)S(1)}, u32[]{:S(2)}, u32[]{:S(2)}) collective-permute-start(f32[64,128]{1,0:T(8,128)S(1)} %get-tuple-element.79), channel_id=1, source_target_pairs={{16,0},{32,16},{48,32},{64,48},{80,64},{96,80},{112,96},{128,112},... | collective-permute-start | bytes 98312 | tf_op jit(solution)/shard_map/while/body/eval_jaxpr/ppermute | solution.py:12
  246.0 6.4 %collective-permute-start = (f32[64,128]{1,0:T(8,128)S(1)}, f32[64,128]{1,0:T(8,128)S(1)}, u32[]{:S(2)}, u32[]{:S(2)}) collective-permute-start(f32[64,128]{1,0:T(8,128)S(1)} %get-tuple-element.79), channel_id=1, source_target_pairs={{16,0},{32,16},{48,32},{64,48},{80,64},{96,80},{112,96},{128,112},... | collective-permute-start | bytes 98312 | tf_op jit(solution)/shard_map/while/body/eval_jaxpr/ppermute | solution.py:12
  254.5 6.4 %collective-permute-start = (f32[64,128]{1,0:T(8,128)S(1)}, f32[64,128]{1,0:T(8,128)S(1)}, u32[]{:S(2)}, u32[]{:S(2)}) collective-permute-start(f32[64,128]{1,0:T(8,128)S(1)} %get-tuple-element.79), channel_id=1, source_target_pairs={{16,0},{32,16},{48,32},{64,48},{80,64},{96,80},{112,96},{128,112},... | collective-permute-start | bytes 98312 | tf_op jit(solution)/shard_map/while/body/eval_jaxpr/ppermute | solution.py:12
  (8 other events, 803.9 us)
Sparse Core Ops, SparseCore 0:
  270.2 137.8 all-reduce.1
where the time goes:
time: 421 us; the launch traced here: 417 us
  waiting for transfers between devices  285 us (68%)
  matrix products  72.4 us (17%)
  starting transfers between devices  41.4 us (10%)
  between operations  15 us (4%)
    ppermute x32, waiting for transfers between devices, passed_along(): return lax.ppermute(x, axis, pairs)  147 us
    psum x1, waiting for transfers between devices, per_device(): summed = lax.psum(whole, 'tile')  138 us
    ppermute x32, starting transfers between devices, passed_along(): return lax.ppermute(x, axis, pairs)  41.3 us
    dot_general x32, matrix products, sweep(): jnp.dot(rhside - jnp.dot(beyond, nextmat, precision=HIGH), inverse, preci...  32.8 us
    dot_general x32, matrix products, sweep(): jnp.dot(beyond, nextmat, precision=HIGH)  32.8 us
  transfers between devices with their start and end apart: 33, of which 33 were waited for; matrix products, arithmetic and copies ran while one was open for 0% of the time, Pallas kernels for 0%

commit v1 on v0

--- a/solution.py
+++ b/solution.py
@@ -4,12 +4,32 @@
 from jax.sharding import PartitionSpec as P
 
 HIGH = lax.Precision.HIGHEST
+REDUCE = "alltoall"
 
 
-def passed_along(x, axis, by):
+def pulled_from(x, axis, by):
     size = lax.axis_size(axis)
-    pairs = [(i, i + by) for i in range(size) if 0 <= i + by < size]
+    pairs = [(i + by, i) for i in range(size) if i + by < size]
     return lax.ppermute(x, axis, pairs)
+
+
+def chain_multipliers(inverse, nextmat, rhside):
+    vectors = rhside.shape[0]
+    b = jnp.dot(rhside, inverse, precision=HIGH)
+    a = -jnp.dot(nextmat, inverse, precision=HIGH)
+    size = lax.axis_size("tm")
+    by = 1
+    while by < size:
+        if by * 2 < size:
+            got = pulled_from(jnp.concatenate([b, a], axis=0), "tm", by)
+            got_b, got_a = got[:vectors], got[vectors:]
+            b = b + jnp.dot(got_b, a, precision=HIGH)
+            a = jnp.dot(got_a, a, precision=HIGH)
+        else:
+            got_b = pulled_from(b, "tm", by)
+            b = b + jnp.dot(got_b, a, precision=HIGH)
+        by *= 2
+    return b
 
 
 def per_device(
@@ -26,16 +46,7 @@
     coupling_next,
     coupling_rhs,
 ):
-    inverse = coupling_inverse[0]
-    nextmat = coupling_next[0]
-    rhside = coupling_rhs[0]
-    start_zero = jnp.zeros(rhside.shape, jnp.float32)
-
-    def sweep(sweep_index, current):
-        beyond = passed_along(current, "tm", -1)
-        return jnp.dot(rhside - jnp.dot(beyond, nextmat, precision=HIGH), inverse, precision=HIGH)
-
-    multipliers = lax.fori_loop(0, lax.axis_size("tm"), sweep, start_zero)
+    multipliers = chain_multipliers(coupling_inverse[0], coupling_next[0], coupling_rhs[0])
     rounded = multipliers.astype(jnp.bfloat16)
     coupled = jnp.einsum(
         "rb,jbc->jrc", rounded, bus_coupling[0], preferred_element_type=jnp.float32
@@ -58,11 +69,18 @@
     )
     products = products * live_mask[:, None, None]
     owned = row_rhs.shape[1]
-    total_rows = owned * lax.axis_size("tile")
+    group = lax.axis_size("tile")
+    total_rows = owned * group
     onehot = (rows[:, None] == jnp.arange(total_rows)[None, :]).astype(jnp.float32)
     whole = jnp.einsum("ki,krc->irc", onehot, products, precision=HIGH)
-    summed = lax.psum(whole, "tile")
-    partials = lax.dynamic_slice_in_dim(summed, lax.axis_index("tile") * owned, owned, 0)
+    if REDUCE == "scatter":
+        partials = lax.psum_scatter(whole, "tile", scatter_dimension=0, tiled=True)
+    elif REDUCE == "alltoall":
+        spread = lax.all_to_all(whole, "tile", 0, 0, tiled=True)
+        partials = spread.reshape((group, owned) + spread.shape[1:]).sum(axis=0)
+    else:
+        summed = lax.psum(whole, "tile")
+        partials = lax.dynamic_slice_in_dim(summed, lax.axis_index("tile") * owned, owned, 0)
     row_work = (row_rhs[0].astype(jnp.float32) - partials).astype(jnp.bfloat16)
     row_values = jnp.einsum(
         "irb,ibc->irc", row_work, row_inverse[0], preferred_element_type=jnp.float32

time: 421 us -> 89.3 us (0.21)
  the two profiles are of different devices: /device:TPU:6 before, /device:TPU:96 now
where the time goes in v1:
time: 89.3 us; the launch traced here: 89 us
  waiting for transfers between devices  45.4 us (51%)
  blocking collectives  23.2 us (26%)
  starting transfers between devices  9.16 us (10%)
  matrix products  8.86 us (10%)
  between operations  1.63 us (2%)
    ppermute x5, waiting for transfers between devices, pulled_from(): return lax.ppermute(x, axis, pairs)  45.4 us
    all_to_all x1, blocking collectives, per_device(): spread = lax.all_to_all(whole, 'tile', 0, 0, tiled=True)  23.2 us
    ppermute x5, starting transfers between devices, pulled_from(): return lax.ppermute(x, axis, pairs)  9.16 us
    dot_general x1, matrix products, per_device(): whole = jnp.einsum('ki,krc->irc', onehot, products, precision=HIGH)  2.04 us
  transfers between devices with their start and end apart: 5, of which 5 were waited for; matrix products, arithmetic and copies ran while one was open for 0% of the time, Pallas kernels for 0%

profile of v1, /device:TPU:96, one launch (start us, length us, event | category | flops | bytes accessed | tf_op | source)
XLA Modules:
  0.0 89.0 jit_solution(1309951729820870113)
XLA Ops:
  0.6 0.0 copy-start
  0.7 1.2 %fusion.25 = f32[64,128]{1,0:T(8,128)S(1)} fusion(f32[1,128,128]{2,1,0:T(8,128)} %param.21, f32[1,64,128]{2,1,0:T(8,128)} %param.23), kind=kOutput, calls=%fused_computation.40 | convolution fusion | flops 12582912 | bytes 131072 | tf_op jit(solution)/shard_map/dot_general | solution.py:18
  1.9 1.1 %convolution_negate_fusion = f32[128,128]{1,0:T(8,128)S(1)} fusion(f32[1,128,128]{2,1,0:T(8,128)} %param.22, f32[1,128,128]{2,1,0:T(8,128)} %param.21), kind=kOutput, calls=%fused_computation.10 | convolution fusion | flops 25182208 | bytes 196608 | tf_op jit(solution)/shard_map/dot_general | solution.py:19
  3.0 1.9 %collective-permute-start = (f32[192,128]{1,0:T(8,128)S(1)}, f32[192,128]{1,0:T(8,128)S(1)}, u32[]{:S(2)}, u32[]{:S(2)}) collective-permute-start(f32[192,128]{1,0:T(8,128)S(1)} %pad_maximum_fusion), channel_id=1, source_target_pairs={{16,0},{32,16},{48,32},{64,48},{80,64},{96,80},{112,96},{128,112},... | collective-permute-start | bytes 294920 | tf_op jit(solution)/shard_map/ppermute | solution.py:13
  4.9 2.2 %collective-permute-done = f32[192,128]{1,0:T(8,128)S(1)} collective-permute-done((f32[192,128]{1,0:T(8,128)S(1)}, f32[192,128]{1,0:T(8,128)S(1)}, u32[]{:S(2)}, u32[]{:S(2)}) %collective-permute-start) | collective-permute-done | bytes 98336 | tf_op jit(solution)/shard_map/ppermute | solution.py:13
  7.1 0.2 convolution_add_fusion.4
  7.3 0.2 fusion.19
  7.5 2.0 %collective-permute-start.1 = (f32[192,128]{1,0:T(8,128)S(1)}, f32[192,128]{1,0:T(8,128)S(1)}, u32[]{:S(2)}, u32[]{:S(2)}) collective-permute-start(f32[192,128]{1,0:T(8,128)S(1)} %pad_maximum_fusion.1), channel_id=1, source_target_pairs={{32,0},{48,16},{64,32},{80,48},{96,64},{112,80},{128,96},{144,112}... | collective-permute-start | bytes 294920 | tf_op jit(solution)/shard_map/ppermute | solution.py:13
  9.5 5.7 %collective-permute-done.1 = f32[192,128]{1,0:T(8,128)S(1)} collective-permute-done((f32[192,128]{1,0:T(8,128)S(1)}, f32[192,128]{1,0:T(8,128)S(1)}, u32[]{:S(2)}, u32[]{:S(2)}) %collective-permute-start.1) | collective-permute-done | bytes 98336 | tf_op jit(solution)/shard_map/ppermute | solution.py:13
  15.2 0.2 convolution_add_fusion.3
  15.4 0.2 fusion.17
  15.7 2.6 %collective-permute-start.2 = (f32[192,128]{1,0:T(8,128)S(1)}, f32[192,128]{1,0:T(8,128)S(1)}, u32[]{:S(2)}, u32[]{:S(2)}) collective-permute-start(f32[192,128]{1,0:T(8,128)S(1)} %pad_maximum_fusion.2), channel_id=1, source_target_pairs={{64,0},{80,16},{96,32},{112,48},{128,64},{144,80},{160,96},{176,11... | collective-permute-start | bytes 294920 | tf_op jit(solution)/shard_map/ppermute | solution.py:13
  19.0 7.8 %collective-permute-done.2 = f32[192,128]{1,0:T(8,128)S(1)} collective-permute-done((f32[192,128]{1,0:T(8,128)S(1)}, f32[192,128]{1,0:T(8,128)S(1)}, u32[]{:S(2)}, u32[]{:S(2)}) %collective-permute-start.2) | collective-permute-done | bytes 98336 | tf_op jit(solution)/shard_map/ppermute | solution.py:13
  26.8 0.2 convolution_add_fusion.2
  27.0 0.2 fusion.15
  27.2 1.3 %collective-permute-start.3 = (f32[192,128]{1,0:T(8,128)S(1)}, f32[192,128]{1,0:T(8,128)S(1)}, u32[]{:S(2)}, u32[]{:S(2)}) collective-permute-start(f32[192,128]{1,0:T(8,128)S(1)} %pad_maximum_fusion.3), channel_id=1, source_target_pairs={{128,0},{144,16},{160,32},{176,48},{192,64},{208,80},{224,96},{240... | collective-permute-start | bytes 294920 | tf_op jit(solution)/shard_map/ppermute | solution.py:13
  28.5 16.6 %collective-permute-done.3 = f32[192,128]{1,0:T(8,128)S(1)} collective-permute-done((f32[192,128]{1,0:T(8,128)S(1)}, f32[192,128]{1,0:T(8,128)S(1)}, u32[]{:S(2)}, u32[]{:S(2)}) %collective-permute-start.3) | collective-permute-done | bytes 98336 | tf_op jit(solution)/shard_map/ppermute | solution.py:13
  45.1 0.2 convolution_add_fusion.1
  45.3 1.3 %collective-permute-start.4 = (f32[64,128]{1,0:T(8,128)S(1)}, f32[64,128]{1,0:T(8,128)S(1)}, u32[]{:S(2)}, u32[]{:S(2)}) collective-permute-start(f32[64,128]{1,0:T(8,128)S(1)} %convolution_add_fusion.1), channel_id=1, source_target_pairs={{256,0},{272,16},{288,32},{304,48},{320,64},{336,80},{352,96},{368... | collective-permute-start | bytes 98312 | tf_op jit(solution)/shard_map/ppermute | solution.py:13
  46.6 0.2 fusion.13
  46.9 13.0 %collective-permute-done.4 = f32[64,128]{1,0:T(8,128)S(1)} collective-permute-done((f32[64,128]{1,0:T(8,128)S(1)}, f32[64,128]{1,0:T(8,128)S(1)}, u32[]{:S(2)}, u32[]{:S(2)}) %collective-permute-start.4) | collective-permute-done | bytes 32800 | tf_op jit(solution)/shard_map/ppermute | solution.py:13
  59.9 0.2 convolution_add_fusion
  60.1 0.3 convolution_convert_fusion
  60.4 0.0 copy-start.1
  60.4 0.5 fusion.11
  61.0 1.3 %fusion = f32[64,64,128]{2,1,0:T(8,128)S(1)} fusion(bf16[1,64,128,128]{3,2,1,0:T(8,128)(2,1)S(1)} %copy-done, bf16[64,64,128]{2,0,1:T(8,128)(2,1)S(1)} %fusion.11), kind=kOutput, calls=%fused_computation | convolution fusion | flops 134217728 | bytes 5242880 | tf_op jit(solution)/shard_map/krb,kbc->krc/dot_general | solution.py:67
  62.2 2.0 %fusion.2 = f32[32,64,128]{2,0,1:T(8,128)S(1)} fusion(f32[64,64,128]{2,1,0:T(8,128)S(1)} %fusion, f32[64]{0:T(128)S(1)} %compare_convert_fusion, s32[64]{0:T(128)S(1)} %bitcast.74), kind=kOutput, calls=%fused_computation.3 | convolution fusion | flops 201852928 | bytes 3146240 | tf_op jit(solution)/shard_map/ki,krc->irc/dot_general | solution.py:75
  64.3 0.6 copy.16
  64.9 23.2 %all_to_all.5 = f32[32,64,128]{2,1,0:T(8,128)S(1)} all-to-all(f32[32,64,128]{2,1,0:T(8,128)S(1)} %copy.16), channel_id=1, replica_groups=mesh['tm'=32,'tile'=16] {'tile'}, dimensions={0} | all-to-all | bytes 2097152 | tf_op jit(solution)/shard_map/all_to_all | solution.py:79
  88.1 0.1 reduce_sum.9
  88.2 0.1 fusion.21
  88.2 0.8 convolution_bitcast_fusion.1
  (23 shorter events, 0.1 us)
Async XLA Ops:
  0.6 60.3 %copy-start = (bf16[1,64,128,128]{3,2,1,0:T(8,128)(2,1)S(1)}, bf16[1,64,128,128]{3,2,1,0:T(8,128)(2,1)}, u32[]{:S(2)}) copy-start(bf16[1,64,128,128]{3,2,1,0:T(8,128)(2,1)} %param.15) | copy-start | bytes 6291460
  0.6 59.4 %copy-start.4 = (bf16[1,8,64,128]{3,2,1,0:T(8,128)(2,1)S(1)}, bf16[1,8,64,128]{3,2,1,0:T(8,128)(2,1)}, u32[]{:S(2)}) copy-start(bf16[1,8,64,128]{3,2,1,0:T(8,128)(2,1)} %param.18) | copy-start | bytes 393220
  0.7 59.4 %copy-start.3 = (bf16[1,8,128,128]{3,2,1,0:T(8,128)(2,1)S(1)}, bf16[1,8,128,128]{3,2,1,0:T(8,128)(2,1)}, u32[]{:S(2)}) copy-start(bf16[1,8,128,128]{3,2,1,0:T(8,128)(2,1)} %param.17) | copy-start | bytes 786436
  0.7 59.4 %copy-start.2 = (bf16[1,8,128,128]{3,2,1,0:T(8,128)(2,1)S(1)}, bf16[1,8,128,128]{3,2,1,0:T(8,128)(2,1)}, u32[]{:S(2)}) copy-start(bf16[1,8,128,128]{3,2,1,0:T(8,128)(2,1)} %param.16) | copy-start | bytes 786436
  0.7 59.8 %copy-start.8 = (s32[1,64]{1,0:T(1,128)S(1)}, s32[1,64]{1,0:T(1,128)}, u32[]{:S(2)}) copy-start(s32[1,64]{1,0:T(1,128)} %param.13) | copy-start | bytes 772
  3.0 4.1 %collective-permute-start = (f32[192,128]{1,0:T(8,128)S(1)}, f32[192,128]{1,0:T(8,128)S(1)}, u32[]{:S(2)}, u32[]{:S(2)}) collective-permute-start(f32[192,128]{1,0:T(8,128)S(1)} %pad_maximum_fusion), channel_id=1, source_target_pairs={{16,0},{32,16},{48,32},{64,48},{80,64},{96,80},{112,96},{128,112},... | collective-permute-start | bytes 294920 | tf_op jit(solution)/shard_map/ppermute | solution.py:13
  7.5 7.7 %collective-permute-start.1 = (f32[192,128]{1,0:T(8,128)S(1)}, f32[192,128]{1,0:T(8,128)S(1)}, u32[]{:S(2)}, u32[]{:S(2)}) collective-permute-start(f32[192,128]{1,0:T(8,128)S(1)} %pad_maximum_fusion.1), channel_id=1, source_target_pairs={{32,0},{48,16},{64,32},{80,48},{96,64},{112,80},{128,96},{144,112}... | collective-permute-start | bytes 294920 | tf_op jit(solution)/shard_map/ppermute | solution.py:13
  15.7 11.1 %collective-permute-start.2 = (f32[192,128]{1,0:T(8,128)S(1)}, f32[192,128]{1,0:T(8,128)S(1)}, u32[]{:S(2)}, u32[]{:S(2)}) collective-permute-start(f32[192,128]{1,0:T(8,128)S(1)} %pad_maximum_fusion.2), channel_id=1, source_target_pairs={{64,0},{80,16},{96,32},{112,48},{128,64},{144,80},{160,96},{176,11... | collective-permute-start | bytes 294920 | tf_op jit(solution)/shard_map/ppermute | solution.py:13
  27.2 17.9 %collective-permute-start.3 = (f32[192,128]{1,0:T(8,128)S(1)}, f32[192,128]{1,0:T(8,128)S(1)}, u32[]{:S(2)}, u32[]{:S(2)}) collective-permute-start(f32[192,128]{1,0:T(8,128)S(1)} %pad_maximum_fusion.3), channel_id=1, source_target_pairs={{128,0},{144,16},{160,32},{176,48},{192,64},{208,80},{224,96},{240... | collective-permute-start | bytes 294920 | tf_op jit(solution)/shard_map/ppermute | solution.py:13
  45.3 14.5 %collective-permute-start.4 = (f32[64,128]{1,0:T(8,128)S(1)}, f32[64,128]{1,0:T(8,128)S(1)}, u32[]{:S(2)}, u32[]{:S(2)}) collective-permute-start(f32[64,128]{1,0:T(8,128)S(1)} %convolution_add_fusion.1), channel_id=1, source_target_pairs={{256,0},{272,16},{288,32},{304,48},{320,64},{336,80},{352,96},{368... | collective-permute-start | bytes 98312 | tf_op jit(solution)/shard_map/ppermute | solution.py:13
  60.1 2.1 %copy-start.5 = (f32[64,128]{1,0:T(8,128)}, f32[64,128]{1,0:T(8,128)S(1)}, u32[]{:S(2)}) copy-start(f32[64,128]{1,0:T(8,128)S(1)} %convolution_add_fusion) | copy-start | bytes 98308
  60.4 1.8 %copy-start.1 = (bf16[8,64,128]{2,1,0:T(8,128)(2,1)}, bf16[8,64,128]{2,1,0:T(8,128)(2,1)S(1)}, u32[]{:S(2)}) copy-start(bf16[8,64,128]{2,1,0:T(8,128)(2,1)S(1)} %convolution_convert_fusion) | copy-start | bytes 393220
  60.9 1.3 %copy-start.9 = (s32[1,64]{1,0:T(1,128)S(1)}, s32[1,64]{1,0:T(1,128)}, u32[]{:S(2)}) copy-start(s32[1,64]{1,0:T(1,128)} %param.12) | copy-start | bytes 772
  64.9 23.3 %copy-start.7 = (bf16[1,2,64,128]{3,2,1,0:T(8,128)(2,1)S(1)}, bf16[1,2,64,128]{3,2,1,0:T(8,128)(2,1)}, u32[]{:S(2)}) copy-start(bf16[1,2,64,128]{3,2,1,0:T(8,128)(2,1)} %param.20) | copy-start | bytes 98308
  64.9 23.3 %copy-start.6 = (bf16[1,2,128,128]{3,2,1,0:T(8,128)(2,1)S(1)}, bf16[1,2,128,128]{3,2,1,0:T(8,128)(2,1)}, u32[]{:S(2)}) copy-start(bf16[1,2,128,128]{3,2,1,0:T(8,128)(2,1)} %param.19) | copy-start | bytes 196612

commit v2 on v1

--- a/solution.py
+++ b/solution.py
@@ -4,7 +4,6 @@
 from jax.sharding import PartitionSpec as P
 
 HIGH = lax.Precision.HIGHEST
-REDUCE = "alltoall"
 
 
 def pulled_from(x, axis, by):
@@ -20,14 +19,16 @@
     size = lax.axis_size("tm")
     by = 1
     while by < size:
+        if by * 4 == size:
+            b = b + jnp.dot(pulled_from(b, "tm", by), a, precision=HIGH)
+            ahead = jnp.dot(pulled_from(b, "tm", by), a, precision=HIGH)
+            b = b + jnp.dot(pulled_from(ahead, "tm", by), a, precision=HIGH)
+            break
+        got = pulled_from(jnp.concatenate([b, a], axis=0), "tm", by)
+        got_b, got_a = got[:vectors], got[vectors:]
+        b = b + jnp.dot(got_b, a, precision=HIGH)
         if by * 2 < size:
-            got = pulled_from(jnp.concatenate([b, a], axis=0), "tm", by)
-            got_b, got_a = got[:vectors], got[vectors:]
-            b = b + jnp.dot(got_b, a, precision=HIGH)
             a = jnp.dot(got_a, a, precision=HIGH)
-        else:
-            got_b = pulled_from(b, "tm", by)
-            b = b + jnp.dot(got_b, a, precision=HIGH)
         by *= 2
     return b
 
@@ -63,24 +64,19 @@
     chosen = jnp.einsum(
         "kj,jrb->krb", select_table, bus_values, preferred_element_type=jnp.float32
     ).astype(jnp.bfloat16)
-    live_mask = (jnp.arange(slots) < live_tiles[0, 0]).astype(jnp.float32)
+    live = jnp.arange(slots) < live_tiles[0, 0]
     products = jnp.einsum(
         "krb,kbc->krc", chosen, factor_tiles[0], preferred_element_type=jnp.float32
     )
-    products = products * live_mask[:, None, None]
     owned = row_rhs.shape[1]
     group = lax.axis_size("tile")
     total_rows = owned * group
-    onehot = (rows[:, None] == jnp.arange(total_rows)[None, :]).astype(jnp.float32)
-    whole = jnp.einsum("ki,krc->irc", onehot, products, precision=HIGH)
-    if REDUCE == "scatter":
-        partials = lax.psum_scatter(whole, "tile", scatter_dimension=0, tiled=True)
-    elif REDUCE == "alltoall":
-        spread = lax.all_to_all(whole, "tile", 0, 0, tiled=True)
-        partials = spread.reshape((group, owned) + spread.shape[1:]).sum(axis=0)
-    else:
-        summed = lax.psum(whole, "tile")
-        partials = lax.dynamic_slice_in_dim(summed, lax.axis_index("tile") * owned, owned, 0)
+    placed_in = (jnp.arange(total_rows)[:, None] == rows[None, :]) & live[None, :]
+    whole = jnp.dot(
+        placed_in.astype(jnp.float32), products.reshape(slots, -1), precision=HIGH
+    ).reshape((total_rows,) + products.shape[1:])
+    spread = lax.all_to_all(whole, "tile", 0, 0, tiled=True)
+    partials = spread.reshape((group, owned) + spread.shape[1:]).sum(axis=0)
     row_work = (row_rhs[0].astype(jnp.float32) - partials).astype(jnp.bfloat16)
     row_values = jnp.einsum(
         "irb,ibc->irc", row_work, row_inverse[0], preferred_element_type=jnp.float32

time: 89.3 us -> 87.5 us (0.980)
  waiting for transfers between devices: 45.4 us -> 43.4 us
  blocking collectives: 23.2 us -> 21.9 us
  starting transfers between devices: 9.16 us -> 10.4 us
    ppermute x5 -> x6, waiting for transfers between devices: 45.4 us -> 43.4 us  [pulled_from(): return lax.ppermute(x, axis, pairs)]
    ppermute x5 -> x6, starting transfers between devices: 9.16 us -> 10.4 us  [pulled_from(): return lax.ppermute(x, axis, pairs)]
    all_to_all x1, blocking collectives: 23.2 us -> 21.9 us  [per_device(): spread = lax.all_to_all(whole, 'tile', 0, 0, tiled=True)]
    dot_general x1 -> x4, matrix products: 2.04 us -> 2.6 us  [the longest x1 2.05 us: per_device(): jnp.dot(placed_in.astype(jnp.float32), products.reshape(slots, -1), preci...]
  transfers between devices with their start and end apart: 5 -> 6, of which waited for: 5 -> 6; matrix products, arithmetic and copies ran while one was open for 0% -> 0% of each run, Pallas kernels for 0% -> 0%
where the time goes in v2:
time: 87.5 us; the launch traced here: 87.1 us
  waiting for transfers between devices  43.4 us (50%)
  blocking collectives  21.9 us (25%)
  starting transfers between devices  10.4 us (12%)
  matrix products  8.84 us (10%)
  between operations  1.63 us (2%)
    ppermute x6, waiting for transfers between devices, pulled_from(): return lax.ppermute(x, axis, pairs)  43.4 us
    all_to_all x1, blocking collectives, per_device(): spread = lax.all_to_all(whole, 'tile', 0, 0, tiled=True)  21.9 us
    ppermute x6, starting transfers between devices, pulled_from(): return lax.ppermute(x, axis, pairs)  10.4 us
    dot_general x1, matrix products, per_device(): jnp.dot(placed_in.astype(jnp.float32), products.reshape(slots, -1), preci...  2.05 us
  transfers between devices with their start and end apart: 6, of which 6 were waited for; matrix products, arithmetic and copies ran while one was open for 0% of the time, Pallas kernels for 0%

profile of v2, /device:TPU:96, one launch (start us, length us, event | category | flops | bytes accessed | tf_op | source)
XLA Modules:
  0.0 87.1 jit_solution(7781719499750404909)
XLA Ops:
  0.7 1.2 %fusion.24 = f32[64,128]{1,0:T(8,128)S(1)} fusion(f32[1,128,128]{2,1,0:T(8,128)} %param.21, f32[1,64,128]{2,1,0:T(8,128)} %param.23), kind=kOutput, calls=%fused_computation.38 | convolution fusion | flops 12582912 | bytes 131072 | tf_op jit(solution)/shard_map/dot_general | solution.py:17
  1.9 1.1 %convolution_negate_fusion = f32[128,128]{1,0:T(8,128)S(1)} fusion(f32[1,128,128]{2,1,0:T(8,128)} %param.22, f32[1,128,128]{2,1,0:T(8,128)} %param.21), kind=kOutput, calls=%fused_computation.12 | convolution fusion | flops 25182208 | bytes 196608 | tf_op jit(solution)/shard_map/dot_general | solution.py:18
  3.0 1.9 %collective-permute-start = (f32[192,128]{1,0:T(8,128)S(1)}, f32[192,128]{1,0:T(8,128)S(1)}, u32[]{:S(2)}, u32[]{:S(2)}) collective-permute-start(f32[192,128]{1,0:T(8,128)S(1)} %pad_maximum_fusion), channel_id=1, source_target_pairs={{16,0},{32,16},{48,32},{64,48},{80,64},{96,80},{112,96},{128,112},... | collective-permute-start | bytes 294920 | tf_op jit(solution)/shard_map/ppermute | solution.py:12
  4.9 2.2 %collective-permute-done = f32[192,128]{1,0:T(8,128)S(1)} collective-permute-done((f32[192,128]{1,0:T(8,128)S(1)}, f32[192,128]{1,0:T(8,128)S(1)}, u32[]{:S(2)}, u32[]{:S(2)}) %collective-permute-start) | collective-permute-done | bytes 98336 | tf_op jit(solution)/shard_map/ppermute | solution.py:12
  7.1 0.2 convolution_add_fusion.4
  7.3 0.2 fusion.18
  7.5 2.0 %collective-permute-start.1 = (f32[192,128]{1,0:T(8,128)S(1)}, f32[192,128]{1,0:T(8,128)S(1)}, u32[]{:S(2)}, u32[]{:S(2)}) collective-permute-start(f32[192,128]{1,0:T(8,128)S(1)} %pad_maximum_fusion.1), channel_id=1, source_target_pairs={{32,0},{48,16},{64,32},{80,48},{96,64},{112,80},{128,96},{144,112}... | collective-permute-start | bytes 294920 | tf_op jit(solution)/shard_map/ppermute | solution.py:12
  9.5 5.7 %collective-permute-done.1 = f32[192,128]{1,0:T(8,128)S(1)} collective-permute-done((f32[192,128]{1,0:T(8,128)S(1)}, f32[192,128]{1,0:T(8,128)S(1)}, u32[]{:S(2)}, u32[]{:S(2)}) %collective-permute-start.1) | collective-permute-done | bytes 98336 | tf_op jit(solution)/shard_map/ppermute | solution.py:12
  15.2 0.2 convolution_add_fusion.3
  15.4 0.2 fusion.16
  15.7 2.6 %collective-permute-start.2 = (f32[192,128]{1,0:T(8,128)S(1)}, f32[192,128]{1,0:T(8,128)S(1)}, u32[]{:S(2)}, u32[]{:S(2)}) collective-permute-start(f32[192,128]{1,0:T(8,128)S(1)} %pad_maximum_fusion.2), channel_id=1, source_target_pairs={{64,0},{80,16},{96,32},{112,48},{128,64},{144,80},{160,96},{176,11... | collective-permute-start | bytes 294920 | tf_op jit(solution)/shard_map/ppermute | solution.py:12
  18.3 8.5 %collective-permute-done.2 = f32[192,128]{1,0:T(8,128)S(1)} collective-permute-done((f32[192,128]{1,0:T(8,128)S(1)}, f32[192,128]{1,0:T(8,128)S(1)}, u32[]{:S(2)}, u32[]{:S(2)}) %collective-permute-start.2) | collective-permute-done | bytes 98336 | tf_op jit(solution)/shard_map/ppermute | solution.py:12
  26.8 0.2 convolution_add_fusion.2
  27.0 1.3 %collective-permute-start.3 = (f32[64,128]{1,0:T(8,128)S(1)}, f32[64,128]{1,0:T(8,128)S(1)}, u32[]{:S(2)}, u32[]{:S(2)}) collective-permute-start(f32[64,128]{1,0:T(8,128)S(1)} %convolution_add_fusion.2), channel_id=1, source_target_pairs={{128,0},{144,16},{160,32},{176,48},{192,64},{208,80},{224,96},{240... | collective-permute-start | bytes 98312 | tf_op jit(solution)/shard_map/ppermute | solution.py:12
  28.3 0.2 fusion.14
  28.5 10.1 %collective-permute-done.3 = f32[64,128]{1,0:T(8,128)S(1)} collective-permute-done((f32[64,128]{1,0:T(8,128)S(1)}, f32[64,128]{1,0:T(8,128)S(1)}, u32[]{:S(2)}, u32[]{:S(2)}) %collective-permute-start.3) | collective-permute-done | bytes 32800 | tf_op jit(solution)/shard_map/ppermute | solution.py:12
  38.6 0.2 convolution_add_fusion.1
  38.8 1.3 %collective-permute-start.4 = (f32[64,128]{1,0:T(8,128)S(1)}, f32[64,128]{1,0:T(8,128)S(1)}, u32[]{:S(2)}, u32[]{:S(2)}) collective-permute-start(f32[64,128]{1,0:T(8,128)S(1)} %convolution_add_fusion.1), channel_id=1, source_target_pairs={{128,0},{144,16},{160,32},{176,48},{192,64},{208,80},{224,96},{240... | collective-permute-start | bytes 98312 | tf_op jit(solution)/shard_map/ppermute | solution.py:12
  40.7 8.6 %collective-permute-done.4 = f32[64,128]{1,0:T(8,128)S(1)} collective-permute-done((f32[64,128]{1,0:T(8,128)S(1)}, f32[64,128]{1,0:T(8,128)S(1)}, u32[]{:S(2)}, u32[]{:S(2)}) %collective-permute-start.4) | collective-permute-done | bytes 32800 | tf_op jit(solution)/shard_map/ppermute | solution.py:12
  49.3 0.2 fusion.43
  49.5 1.3 %collective-permute-start.5 = (f32[64,128]{1,0:T(8,128)S(1)}, f32[64,128]{1,0:T(8,128)S(1)}, u32[]{:S(2)}, u32[]{:S(2)}) collective-permute-start(f32[64,128]{1,0:T(8,128)S(1)} %fusion.43), channel_id=1, source_target_pairs={{128,0},{144,16},{160,32},{176,48},{192,64},{208,80},{224,96},{240... | collective-permute-start | bytes 98312 | tf_op jit(solution)/shard_map/ppermute | solution.py:12
  50.8 8.4 %collective-permute-done.5 = f32[64,128]{1,0:T(8,128)S(1)} collective-permute-done((f32[64,128]{1,0:T(8,128)S(1)}, f32[64,128]{1,0:T(8,128)S(1)}, u32[]{:S(2)}, u32[]{:S(2)}) %collective-permute-start.5) | collective-permute-done | bytes 32800 | tf_op jit(solution)/shard_map/ppermute | solution.py:12
  59.2 0.2 convolution_add_fusion
  59.4 0.3 convolution_convert_fusion.1
  59.8 0.5 convolution_convert_fusion
  60.3 1.3 %fusion.3 = f32[64,64,128]{2,1,0:T(8,128)S(1)} fusion(bf16[1,64,128,128]{3,2,1,0:T(8,128)(2,1)S(1)} %copy-done, bf16[64,64,128]{2,0,1:T(8,128)(2,1)S(1)} %convolution_convert_fusion), kind=kOutput, calls=%fused_computation.4 | convolution fusion | flops 134217728 | bytes 5242880 | tf_op jit(solution)/shard_map/krb,kbc->krc/dot_general | solution.py:68
  61.6 2.1 %fusion = f32[32,64,128]{2,0,1:T(8,128)S(1)} fusion(s32[64]{0:T(128)S(1)} %bitcast.90, pred[64]{0:T(512)(128)(4,1)S(1)} %iota_compare_fusion.2, f32[8,8,64,128]{3,2,1,0:T(8,128)S(1)} %bitcast.85), kind=kOutput, calls=%fused_computation.1 | convolution fusion | flops 201330688 | bytes 3146048 | tf_op jit(solution)/shard_map/dot_general | solution.py:75
  63.6 0.6 copy.20
  64.3 21.9 %all_to_all.5 = f32[32,64,128]{2,1,0:T(8,128)S(1)} all-to-all(f32[32,64,128]{2,1,0:T(8,128)S(1)} %copy.20), channel_id=1, replica_groups=mesh['tm'=32,'tile'=16] {'tile'}, dimensions={0} | all-to-all | bytes 2097152 | tf_op jit(solution)/shard_map/all_to_all | solution.py:78
  86.2 0.1 reduce_sum.9
  86.2 0.1 fusion.20
  86.3 0.8 convolution_bitcast_fusion.1
  (24 shorter events, 0.1 us)
Async XLA Ops:
  0.6 59.6 %copy-start = (bf16[1,64,128,128]{3,2,1,0:T(8,128)(2,1)S(1)}, bf16[1,64,128,128]{3,2,1,0:T(8,128)(2,1)}, u32[]{:S(2)}) copy-start(bf16[1,64,128,128]{3,2,1,0:T(8,128)(2,1)} %param.15) | copy-start | bytes 6291460
  0.6 58.7 %copy-start.4 = (bf16[1,8,64,128]{3,2,1,0:T(8,128)(2,1)S(1)}, bf16[1,8,64,128]{3,2,1,0:T(8,128)(2,1)}, u32[]{:S(2)}) copy-start(bf16[1,8,64,128]{3,2,1,0:T(8,128)(2,1)} %param.18) | copy-start | bytes 393220
  0.7 58.7 %copy-start.3 = (bf16[1,8,128,128]{3,2,1,0:T(8,128)(2,1)S(1)}, bf16[1,8,128,128]{3,2,1,0:T(8,128)(2,1)}, u32[]{:S(2)}) copy-start(bf16[1,8,128,128]{3,2,1,0:T(8,128)(2,1)} %param.17) | copy-start | bytes 786436
  0.7 58.7 %copy-start.2 = (bf16[1,8,128,128]{3,2,1,0:T(8,128)(2,1)S(1)}, bf16[1,8,128,128]{3,2,1,0:T(8,128)(2,1)}, u32[]{:S(2)}) copy-start(bf16[1,8,128,128]{3,2,1,0:T(8,128)(2,1)} %param.16) | copy-start | bytes 786436
  0.7 59.1 %copy-start.8 = (s32[1,64]{1,0:T(1,128)S(1)}, s32[1,64]{1,0:T(1,128)}, u32[]{:S(2)}) copy-start(s32[1,64]{1,0:T(1,128)} %param.13) | copy-start | bytes 772
  3.0 4.1 %collective-permute-start = (f32[192,128]{1,0:T(8,128)S(1)}, f32[192,128]{1,0:T(8,128)S(1)}, u32[]{:S(2)}, u32[]{:S(2)}) collective-permute-start(f32[192,128]{1,0:T(8,128)S(1)} %pad_maximum_fusion), channel_id=1, source_target_pairs={{16,0},{32,16},{48,32},{64,48},{80,64},{96,80},{112,96},{128,112},... | collective-permute-start | bytes 294920 | tf_op jit(solution)/shard_map/ppermute | solution.py:12
  7.5 7.7 %collective-permute-start.1 = (f32[192,128]{1,0:T(8,128)S(1)}, f32[192,128]{1,0:T(8,128)S(1)}, u32[]{:S(2)}, u32[]{:S(2)}) collective-permute-start(f32[192,128]{1,0:T(8,128)S(1)} %pad_maximum_fusion.1), channel_id=1, source_target_pairs={{32,0},{48,16},{64,32},{80,48},{96,64},{112,80},{128,96},{144,112}... | collective-permute-start | bytes 294920 | tf_op jit(solution)/shard_map/ppermute | solution.py:12
  15.7 11.1 %collective-permute-start.2 = (f32[192,128]{1,0:T(8,128)S(1)}, f32[192,128]{1,0:T(8,128)S(1)}, u32[]{:S(2)}, u32[]{:S(2)}) collective-permute-start(f32[192,128]{1,0:T(8,128)S(1)} %pad_maximum_fusion.2), channel_id=1, source_target_pairs={{64,0},{80,16},{96,32},{112,48},{128,64},{144,80},{160,96},{176,11... | collective-permute-start | bytes 294920 | tf_op jit(solution)/shard_map/ppermute | solution.py:12
  27.0 11.6 %collective-permute-start.3 = (f32[64,128]{1,0:T(8,128)S(1)}, f32[64,128]{1,0:T(8,128)S(1)}, u32[]{:S(2)}, u32[]{:S(2)}) collective-permute-start(f32[64,128]{1,0:T(8,128)S(1)} %convolution_add_fusion.2), channel_id=1, source_target_pairs={{128,0},{144,16},{160,32},{176,48},{192,64},{208,80},{224,96},{240... | collective-permute-start | bytes 98312 | tf_op jit(solution)/shard_map/ppermute | solution.py:12
  38.8 10.5 %collective-permute-start.4 = (f32[64,128]{1,0:T(8,128)S(1)}, f32[64,128]{1,0:T(8,128)S(1)}, u32[]{:S(2)}, u32[]{:S(2)}) collective-permute-start(f32[64,128]{1,0:T(8,128)S(1)} %convolution_add_fusion.1), channel_id=1, source_target_pairs={{128,0},{144,16},{160,32},{176,48},{192,64},{208,80},{224,96},{240... | collective-permute-start | bytes 98312 | tf_op jit(solution)/shard_map/ppermute | solution.py:12
  49.5 9.7 %collective-permute-start.5 = (f32[64,128]{1,0:T(8,128)S(1)}, f32[64,128]{1,0:T(8,128)S(1)}, u32[]{:S(2)}, u32[]{:S(2)}) collective-permute-start(f32[64,128]{1,0:T(8,128)S(1)} %fusion.43), channel_id=1, source_target_pairs={{128,0},{144,16},{160,32},{176,48},{192,64},{208,80},{224,96},{240... | collective-permute-start | bytes 98312 | tf_op jit(solution)/shard_map/ppermute | solution.py:12
  59.4 2.1 %copy-start.5 = (f32[64,128]{1,0:T(8,128)}, f32[64,128]{1,0:T(8,128)S(1)}, u32[]{:S(2)}) copy-start(f32[64,128]{1,0:T(8,128)S(1)} %convolution_add_fusion) | copy-start | bytes 98308
  59.8 1.8 %copy-start.1 = (bf16[8,64,128]{2,1,0:T(8,128)(2,1)}, bf16[8,64,128]{2,1,0:T(8,128)(2,1)S(1)}, u32[]{:S(2)}) copy-start(bf16[8,64,128]{2,1,0:T(8,128)(2,1)S(1)} %convolution_convert_fusion.1) | copy-start | bytes 393220
  60.3 1.3 %copy-start.9 = (s32[1,64]{1,0:T(1,128)S(1)}, s32[1,64]{1,0:T(1,128)}, u32[]{:S(2)}) copy-start(s32[1,64]{1,0:T(1,128)} %param.12) | copy-start | bytes 772
  64.2 22.0 %copy-start.7 = (bf16[1,2,64,128]{3,2,1,0:T(8,128)(2,1)S(1)}, bf16[1,2,64,128]{3,2,1,0:T(8,128)(2,1)}, u32[]{:S(2)}) copy-start(bf16[1,2,64,128]{3,2,1,0:T(8,128)(2,1)} %param.20) | copy-start | bytes 98308
  64.3 22.1 %copy-start.6 = (bf16[1,2,128,128]{3,2,1,0:T(8,128)(2,1)S(1)}, bf16[1,2,128,128]{3,2,1,0:T(8,128)(2,1)}, u32[]{:S(2)}) copy-start(bf16[1,2,128,128]{3,2,1,0:T(8,128)(2,1)} %param.19) | copy-start | bytes 196612

commit v3 on v2

--- a/solution.py
+++ b/solution.py
@@ -18,6 +18,15 @@
     a = -jnp.dot(nextmat, inverse, precision=HIGH)
     size = lax.axis_size("tm")
     by = 1
+    if size >= 8:
+        held = jnp.concatenate([b, a], axis=0)
+        got = [pulled_from(held, "tm", k) for k in (1, 2, 3)]
+        carry = got[2]
+        for step in (got[1], got[0], held):
+            carry = jnp.dot(carry, step[vectors:], precision=HIGH)
+            carry = carry.at[:vectors].add(step[:vectors])
+        b, a = carry[:vectors], carry[vectors:]
+        by = 4
     while by < size:
         if by * 4 == size:
             b = b + jnp.dot(pulled_from(b, "tm", by), a, precision=HIGH)

time: 87.5 us -> 85 us (0.971)
  waiting for transfers between devices: 43.4 us -> 35.2 us
  starting transfers between devices: 10.4 us -> 16.9 us
    ppermute x6 -> x7, waiting for transfers between devices: 43.4 us -> 35.2 us  [pulled_from(): return lax.ppermute(x, axis, pairs)]
    ppermute x6 -> x7, starting transfers between devices: 10.4 us -> 16.9 us  [pulled_from(): return lax.ppermute(x, axis, pairs)]
  transfers between devices with their start and end apart: 6 -> 7, of which waited for: 6 -> 5; matrix products, arithmetic and copies ran while one was open for 0% -> 1% of each run, Pallas kernels for 0% -> 0%
where the time goes in v3:
time: 85 us; the launch traced here: 84.6 us
  waiting for transfers between devices  35.2 us (41%)
  blocking collectives  21.2 us (25%)
  starting transfers between devices  16.9 us (20%)
  matrix products  8.77 us (10%)
  between operations  1.66 us (2%)
    ppermute x7, waiting for transfers between devices, pulled_from(): return lax.ppermute(x, axis, pairs)  35.2 us
    all_to_all x1, blocking collectives, per_device(): spread = lax.all_to_all(whole, 'tile', 0, 0, tiled=True)  21.2 us
    ppermute x7, starting transfers between devices, pulled_from(): return lax.ppermute(x, axis, pairs)  16.9 us
    dot_general x1, matrix products, per_device(): jnp.dot(placed_in.astype(jnp.float32), products.reshape(slots, -1), preci...  2.05 us
  transfers between devices with their start and end apart: 7, of which 5 were waited for; matrix products, arithmetic and copies ran while one was open for 1% of the time, Pallas kernels for 0%

profile of v3, /device:TPU:96, one launch (start us, length us, event | category | flops | bytes accessed | tf_op | source)
XLA Modules:
  0.0 84.6 jit_solution(13593064043114028718)
XLA Ops:
  0.6 0.0 copy-start
  0.7 1.2 %fusion.24 = f32[64,128]{1,0:T(8,128)S(1)} fusion(f32[1,128,128]{2,1,0:T(8,128)} %param.27, f32[1,64,128]{2,1,0:T(8,128)} %param.29), kind=kOutput, calls=%fused_computation.34 | convolution fusion | flops 12582912 | bytes 131072 | tf_op jit(solution)/shard_map/dot_general | solution.py:17
  1.9 1.1 %convolution_negate_fusion = f32[128,128]{1,0:T(8,128)S(1)} fusion(f32[1,128,128]{2,1,0:T(8,128)} %param.28, f32[1,128,128]{2,1,0:T(8,128)} %param.27), kind=kOutput, calls=%fused_computation.12 | convolution fusion | flops 25182208 | bytes 196608 | tf_op jit(solution)/shard_map/dot_general | solution.py:18
  3.0 2.0 %collective-permute-start.1 = (f32[192,128]{1,0:T(8,128)S(1)}, f32[192,128]{1,0:T(8,128)S(1)}, u32[]{:S(2)}, u32[]{:S(2)}) collective-permute-start(f32[192,128]{1,0:T(8,128)S(1)} %pad_maximum_fusion), channel_id=1, source_target_pairs={{32,0},{48,16},{64,32},{80,48},{96,64},{112,80},{128,96},{144,112}... | collective-permute-start | bytes 294920 | tf_op jit(solution)/shard_map/ppermute | solution.py:12
  5.0 1.9 %collective-permute-start = (f32[192,128]{1,0:T(8,128)S(1)}, f32[192,128]{1,0:T(8,128)S(1)}, u32[]{:S(2)}, u32[]{:S(2)}) collective-permute-start(f32[192,128]{1,0:T(8,128)S(1)} %pad_maximum_fusion), channel_id=1, source_target_pairs={{48,0},{64,16},{80,32},{96,48},{112,64},{128,80},{144,96},{160,112... | collective-permute-start | bytes 294920 | tf_op jit(solution)/shard_map/ppermute | solution.py:12
  6.9 7.2 %collective-permute-start.2 = (f32[192,128]{1,0:T(8,128)S(1)}, f32[192,128]{1,0:T(8,128)S(1)}, u32[]{:S(2)}, u32[]{:S(2)}) collective-permute-start(f32[192,128]{1,0:T(8,128)S(1)} %pad_maximum_fusion), channel_id=1, source_target_pairs={{16,0},{32,16},{48,32},{64,48},{80,64},{96,80},{112,96},{128,112},... | collective-permute-start | bytes 294920 | tf_op jit(solution)/shard_map/ppermute | solution.py:12
  14.1 0.2 fusion.18
  14.4 1.9 %collective-permute-done.2 = f32[192,128]{1,0:T(8,128)S(1)} collective-permute-done((f32[192,128]{1,0:T(8,128)S(1)}, f32[192,128]{1,0:T(8,128)S(1)}, u32[]{:S(2)}, u32[]{:S(2)}) %collective-permute-start.2) | collective-permute-done | bytes 98336 | tf_op jit(solution)/shard_map/ppermute | solution.py:12
  16.3 0.2 fusion.16
  16.6 0.2 fusion.46
  16.8 1.9 %collective-permute-start.3 = (f32[192,128]{1,0:T(8,128)S(1)}, f32[192,128]{1,0:T(8,128)S(1)}, u32[]{:S(2)}, u32[]{:S(2)}) collective-permute-start(f32[192,128]{1,0:T(8,128)S(1)} %fusion.40), channel_id=1, source_target_pairs={{64,0},{80,16},{96,32},{112,48},{128,64},{144,80},{160,96},{176,11... | collective-permute-start | bytes 294920 | tf_op jit(solution)/shard_map/ppermute | solution.py:12
  18.8 7.5 %collective-permute-done.3 = f32[192,128]{1,0:T(8,128)S(1)} collective-permute-done((f32[192,128]{1,0:T(8,128)S(1)}, f32[192,128]{1,0:T(8,128)S(1)}, u32[]{:S(2)}, u32[]{:S(2)}) %collective-permute-start.3) | collective-permute-done | bytes 98336 | tf_op jit(solution)/shard_map/ppermute | solution.py:12
  26.3 0.2 convolution_add_fusion.2
  26.5 1.3 %collective-permute-start.4 = (f32[64,128]{1,0:T(8,128)S(1)}, f32[64,128]{1,0:T(8,128)S(1)}, u32[]{:S(2)}, u32[]{:S(2)}) collective-permute-start(f32[64,128]{1,0:T(8,128)S(1)} %convolution_add_fusion.2), channel_id=1, source_target_pairs={{128,0},{144,16},{160,32},{176,48},{192,64},{208,80},{224,96},{240... | collective-permute-start | bytes 98312 | tf_op jit(solution)/shard_map/ppermute | solution.py:12
  27.8 0.2 fusion.14
  28.0 8.4 %collective-permute-done.4 = f32[64,128]{1,0:T(8,128)S(1)} collective-permute-done((f32[64,128]{1,0:T(8,128)S(1)}, f32[64,128]{1,0:T(8,128)S(1)}, u32[]{:S(2)}, u32[]{:S(2)}) %collective-permute-start.4) | collective-permute-done | bytes 32800 | tf_op jit(solution)/shard_map/ppermute | solution.py:12
  36.4 0.2 convolution_add_fusion.1
  36.6 1.3 %collective-permute-start.5 = (f32[64,128]{1,0:T(8,128)S(1)}, f32[64,128]{1,0:T(8,128)S(1)}, u32[]{:S(2)}, u32[]{:S(2)}) collective-permute-start(f32[64,128]{1,0:T(8,128)S(1)} %convolution_add_fusion.1), channel_id=1, source_target_pairs={{128,0},{144,16},{160,32},{176,48},{192,64},{208,80},{224,96},{240... | collective-permute-start | bytes 98312 | tf_op jit(solution)/shard_map/ppermute | solution.py:12
  38.6 7.9 %collective-permute-done.5 = f32[64,128]{1,0:T(8,128)S(1)} collective-permute-done((f32[64,128]{1,0:T(8,128)S(1)}, f32[64,128]{1,0:T(8,128)S(1)}, u32[]{:S(2)}, u32[]{:S(2)}) %collective-permute-start.5) | collective-permute-done | bytes 32800 | tf_op jit(solution)/shard_map/ppermute | solution.py:12
  46.4 0.2 fusion.47
  46.6 1.3 %collective-permute-start.6 = (f32[64,128]{1,0:T(8,128)S(1)}, f32[64,128]{1,0:T(8,128)S(1)}, u32[]{:S(2)}, u32[]{:S(2)}) collective-permute-start(f32[64,128]{1,0:T(8,128)S(1)} %fusion.47), channel_id=1, source_target_pairs={{128,0},{144,16},{160,32},{176,48},{192,64},{208,80},{224,96},{240... | collective-permute-start | bytes 98312 | tf_op jit(solution)/shard_map/ppermute | solution.py:12
  47.9 9.5 %collective-permute-done.6 = f32[64,128]{1,0:T(8,128)S(1)} collective-permute-done((f32[64,128]{1,0:T(8,128)S(1)}, f32[64,128]{1,0:T(8,128)S(1)}, u32[]{:S(2)}, u32[]{:S(2)}) %collective-permute-start.6) | collective-permute-done | bytes 32800 | tf_op jit(solution)/shard_map/ppermute | solution.py:12
  57.4 0.2 convolution_add_fusion
  57.6 0.3 convolution_convert_fusion.1
  58.0 0.5 convolution_convert_fusion
  58.5 1.3 %fusion.3 = f32[64,64,128]{2,1,0:T(8,128)S(1)} fusion(bf16[1,64,128,128]{3,2,1,0:T(8,128)(2,1)S(1)} %copy-done, bf16[64,64,128]{2,0,1:T(8,128)(2,1)S(1)} %convolution_convert_fusion), kind=kOutput, calls=%fused_computation.4 | convolution fusion | flops 134217728 | bytes 5242880 | tf_op jit(solution)/shard_map/krb,kbc->krc/dot_general | solution.py:77
  59.8 2.1 %fusion = f32[32,64,128]{2,0,1:T(8,128)S(1)} fusion(s32[64]{0:T(128)S(1)} %bitcast.88, pred[64]{0:T(512)(128)(4,1)S(1)} %iota_compare_fusion.2, f32[8,8,64,128]{3,2,1,0:T(8,128)S(1)} %bitcast.83), kind=kOutput, calls=%fused_computation.1 | convolution fusion | flops 201330688 | bytes 3146048 | tf_op jit(solution)/shard_map/dot_general | solution.py:84
  61.8 0.6 copy.20
  62.5 21.2 %all_to_all.5 = f32[32,64,128]{2,1,0:T(8,128)S(1)} all-to-all(f32[32,64,128]{2,1,0:T(8,128)S(1)} %copy.20), channel_id=1, replica_groups=mesh['tm'=32,'tile'=16] {'tile'}, dimensions={0} | all-to-all | bytes 2097152 | tf_op jit(solution)/shard_map/all_to_all | solution.py:87
  83.7 0.1 reduce_sum.9
  83.7 0.1 fusion.20
  83.8 0.8 convolution_bitcast_fusion.1
  (27 shorter events, 0.1 us)
Async XLA Ops:
  0.6 57.8 %copy-start = (bf16[1,64,128,128]{3,2,1,0:T(8,128)(2,1)S(1)}, bf16[1,64,128,128]{3,2,1,0:T(8,128)(2,1)}, u32[]{:S(2)}) copy-start(bf16[1,64,128,128]{3,2,1,0:T(8,128)(2,1)} %param.21) | copy-start | bytes 6291460
  0.6 56.9 %copy-start.4 = (bf16[1,8,64,128]{3,2,1,0:T(8,128)(2,1)S(1)}, bf16[1,8,64,128]{3,2,1,0:T(8,128)(2,1)}, u32[]{:S(2)}) copy-start(bf16[1,8,64,128]{3,2,1,0:T(8,128)(2,1)} %param.24) | copy-start | bytes 393220
  0.7 56.9 %copy-start.3 = (bf16[1,8,128,128]{3,2,1,0:T(8,128)(2,1)S(1)}, bf16[1,8,128,128]{3,2,1,0:T(8,128)(2,1)}, u32[]{:S(2)}) copy-start(bf16[1,8,128,128]{3,2,1,0:T(8,128)(2,1)} %param.23) | copy-start | bytes 786436
  0.7 56.9 %copy-start.2 = (bf16[1,8,128,128]{3,2,1,0:T(8,128)(2,1)S(1)}, bf16[1,8,128,128]{3,2,1,0:T(8,128)(2,1)}, u32[]{:S(2)}) copy-start(bf16[1,8,128,128]{3,2,1,0:T(8,128)(2,1)} %param.22) | copy-start | bytes 786436
  0.7 57.3 %copy-start.8 = (s32[1,64]{1,0:T(1,128)S(1)}, s32[1,64]{1,0:T(1,128)}, u32[]{:S(2)}) copy-start(s32[1,64]{1,0:T(1,128)} %param.19) | copy-start | bytes 772
  3.0 11.1 %collective-permute-start.1 = (f32[192,128]{1,0:T(8,128)S(1)}, f32[192,128]{1,0:T(8,128)S(1)}, u32[]{:S(2)}, u32[]{:S(2)}) collective-permute-start(f32[192,128]{1,0:T(8,128)S(1)} %pad_maximum_fusion), channel_id=1, source_target_pairs={{32,0},{48,16},{64,32},{80,48},{96,64},{112,80},{128,96},{144,112}... | collective-permute-start | bytes 294920 | tf_op jit(solution)/shard_map/ppermute | solution.py:12
  5.0 9.1 %collective-permute-start = (f32[192,128]{1,0:T(8,128)S(1)}, f32[192,128]{1,0:T(8,128)S(1)}, u32[]{:S(2)}, u32[]{:S(2)}) collective-permute-start(f32[192,128]{1,0:T(8,128)S(1)} %pad_maximum_fusion), channel_id=1, source_target_pairs={{48,0},{64,16},{80,32},{96,48},{112,64},{128,80},{144,96},{160,112... | collective-permute-start | bytes 294920 | tf_op jit(solution)/shard_map/ppermute | solution.py:12
  6.9 9.4 %collective-permute-start.2 = (f32[192,128]{1,0:T(8,128)S(1)}, f32[192,128]{1,0:T(8,128)S(1)}, u32[]{:S(2)}, u32[]{:S(2)}) collective-permute-start(f32[192,128]{1,0:T(8,128)S(1)} %pad_maximum_fusion), channel_id=1, source_target_pairs={{16,0},{32,16},{48,32},{64,48},{80,64},{96,80},{112,96},{128,112},... | collective-permute-start | bytes 294920 | tf_op jit(solution)/shard_map/ppermute | solution.py:12
  16.8 9.4 %collective-permute-start.3 = (f32[192,128]{1,0:T(8,128)S(1)}, f32[192,128]{1,0:T(8,128)S(1)}, u32[]{:S(2)}, u32[]{:S(2)}) collective-permute-start(f32[192,128]{1,0:T(8,128)S(1)} %fusion.40), channel_id=1, source_target_pairs={{64,0},{80,16},{96,32},{112,48},{128,64},{144,80},{160,96},{176,11... | collective-permute-start | bytes 294920 | tf_op jit(solution)/shard_map/ppermute | solution.py:12
  26.5 10.0 %collective-permute-start.4 = (f32[64,128]{1,0:T(8,128)S(1)}, f32[64,128]{1,0:T(8,128)S(1)}, u32[]{:S(2)}, u32[]{:S(2)}) collective-permute-start(f32[64,128]{1,0:T(8,128)S(1)} %convolution_add_fusion.2), channel_id=1, source_target_pairs={{128,0},{144,16},{160,32},{176,48},{192,64},{208,80},{224,96},{240... | collective-permute-start | bytes 98312 | tf_op jit(solution)/shard_map/ppermute | solution.py:12
  36.6 9.8 %collective-permute-start.5 = (f32[64,128]{1,0:T(8,128)S(1)}, f32[64,128]{1,0:T(8,128)S(1)}, u32[]{:S(2)}, u32[]{:S(2)}) collective-permute-start(f32[64,128]{1,0:T(8,128)S(1)} %convolution_add_fusion.1), channel_id=1, source_target_pairs={{128,0},{144,16},{160,32},{176,48},{192,64},{208,80},{224,96},{240... | collective-permute-start | bytes 98312 | tf_op jit(solution)/shard_map/ppermute | solution.py:12
  46.6 10.8 %collective-permute-start.6 = (f32[64,128]{1,0:T(8,128)S(1)}, f32[64,128]{1,0:T(8,128)S(1)}, u32[]{:S(2)}, u32[]{:S(2)}) collective-permute-start(f32[64,128]{1,0:T(8,128)S(1)} %fusion.47), channel_id=1, source_target_pairs={{128,0},{144,16},{160,32},{176,48},{192,64},{208,80},{224,96},{240... | collective-permute-start | bytes 98312 | tf_op jit(solution)/shard_map/ppermute | solution.py:12
  57.6 2.1 %copy-start.5 = (f32[64,128]{1,0:T(8,128)}, f32[64,128]{1,0:T(8,128)S(1)}, u32[]{:S(2)}) copy-start(f32[64,128]{1,0:T(8,128)S(1)} %convolution_add_fusion) | copy-start | bytes 98308
  57.9 1.8 %copy-start.1 = (bf16[8,64,128]{2,1,0:T(8,128)(2,1)}, bf16[8,64,128]{2,1,0:T(8,128)(2,1)S(1)}, u32[]{:S(2)}) copy-start(bf16[8,64,128]{2,1,0:T(8,128)(2,1)S(1)} %convolution_convert_fusion.1) | copy-start | bytes 393220
  58.5 1.3 %copy-start.9 = (s32[1,64]{1,0:T(1,128)S(1)}, s32[1,64]{1,0:T(1,128)}, u32[]{:S(2)}) copy-start(s32[1,64]{1,0:T(1,128)} %param.18) | copy-start | bytes 772
  62.4 21.3 %copy-start.7 = (bf16[1,2,64,128]{3,2,1,0:T(8,128)(2,1)S(1)}, bf16[1,2,64,128]{3,2,1,0:T(8,128)(2,1)}, u32[]{:S(2)}) copy-start(bf16[1,2,64,128]{3,2,1,0:T(8,128)(2,1)} %param.26) | copy-start | bytes 98308
  62.4 21.4 %copy-start.6 = (bf16[1,2,128,128]{3,2,1,0:T(8,128)(2,1)S(1)}, bf16[1,2,128,128]{3,2,1,0:T(8,128)(2,1)}, u32[]{:S(2)}) copy-start(bf16[1,2,128,128]{3,2,1,0:T(8,128)(2,1)} %param.25) | copy-start | bytes 196612

commit v4 on v3

--- a/solution.py
+++ b/solution.py
@@ -4,6 +4,7 @@
 from jax.sharding import PartitionSpec as P
 
 HIGH = lax.Precision.HIGHEST
+MID = lax.Precision.HIGH
 
 
 def pulled_from(x, axis, by):
@@ -14,8 +15,8 @@
 
 def chain_multipliers(inverse, nextmat, rhside):
     vectors = rhside.shape[0]
-    b = jnp.dot(rhside, inverse, precision=HIGH)
-    a = -jnp.dot(nextmat, inverse, precision=HIGH)
+    b = jnp.dot(rhside, inverse, precision=MID)
+    a = -jnp.dot(nextmat, inverse, precision=MID)
     size = lax.axis_size("tm")
     by = 1
     if size >= 8:
@@ -68,11 +69,7 @@
     rows = tile_rows[0]
     cols = tile_cols[0]
     slots = rows.shape[0]
-    buses_here = bus_values.shape[0]
-    select_table = (cols[:, None] == jnp.arange(buses_here)[None, :]).astype(jnp.bfloat16)
-    chosen = jnp.einsum(
-        "kj,jrb->krb", select_table, bus_values, preferred_element_type=jnp.float32
-    ).astype(jnp.bfloat16)
+    chosen = jnp.take(bus_values, cols, axis=0)
     live = jnp.arange(slots) < live_tiles[0, 0]
     products = jnp.einsum(
         "krb,kbc->krc", chosen, factor_tiles[0], preferred_element_type=jnp.float32
@@ -82,7 +79,7 @@
     total_rows = owned * group
     placed_in = (jnp.arange(total_rows)[:, None] == rows[None, :]) & live[None, :]
     whole = jnp.dot(
-        placed_in.astype(jnp.float32), products.reshape(slots, -1), precision=HIGH
+        placed_in.astype(jnp.float32), products.reshape(slots, -1), precision=MID
     ).reshape((total_rows,) + products.shape[1:])
     spread = lax.all_to_all(whole, "tile", 0, 0, tiled=True)
     partials = spread.reshape((group, owned) + spread.shape[1:]).sum(axis=0)

time: 85 us -> 84.3 us (level)
  matrix products: 8.77 us -> 7.37 us
  other arithmetic: 0.17 us -> 1.5 us
  waiting for transfers between devices: 35.2 us -> 33.9 us
    ppermute x7, waiting for transfers between devices: 35.2 us -> 33.9 us  [pulled_from(): return lax.ppermute(x, axis, pairs)]
    dot_general x3 -> x2, matrix products: 2.74 us -> 2.22 us  [the longest x1 1.17 us: chain_multipliers(): b = jnp.dot(rhside, inverse, precision=MID)]
  transfers between devices with their start and end apart: 7 -> 7, of which waited for: 5 -> 5; matrix products, arithmetic and copies ran while one was open for 1% -> 2% of each run, Pallas kernels for 0% -> 0%
where the time goes in v4:
time: 84.3 us; the launch traced here: 83.9 us
  waiting for transfers between devices  33.9 us (40%)
  blocking collectives  21.2 us (25%)
  starting transfers between devices  16.9 us (20%)
  matrix products  7.37 us (9%)
  between operations  1.66 us (2%)
  other arithmetic  1.5 us (2%)
  local copies, waits for them, and re-layouts  1.43 us (2%)
    ppermute x7, waiting for transfers between devices, pulled_from(): return lax.ppermute(x, axis, pairs)  33.9 us
    all_to_all x1, blocking collectives, per_device(): spread = lax.all_to_all(whole, 'tile', 0, 0, tiled=True)  21.2 us
    ppermute x7, starting transfers between devices, pulled_from(): return lax.ppermute(x, axis, pairs)  16.9 us
    dot_general x1, matrix products, per_device(): jnp.dot(placed_in.astype(jnp.float32), products.reshape(slots, -1), preci...  1.7 us
  transfers between devices with their start and end apart: 7, of which 5 were waited for; matrix products, arithmetic and copies ran while one was open for 2% of the time, Pallas kernels for 0%

profile of v4, /device:TPU:96, one launch (start us, length us, event | category | flops | bytes accessed | tf_op | source)
XLA Modules:
  0.0 83.9 jit_solution(2967574945814195987)
XLA Ops:
  0.7 1.2 %fusion.25 = f32[64,128]{1,0:T(8,128)S(1)} fusion(f32[1,128,128]{2,1,0:T(8,128)} %param.27, f32[1,64,128]{2,1,0:T(8,128)} %param.29), kind=kOutput, calls=%fused_computation.35 | convolution fusion | flops 6291456 | bytes 131072 | tf_op jit(solution)/shard_map/dot_general | solution.py:18
  1.9 1.0 %convolution_negate_fusion = f32[128,128]{1,0:T(8,128)S(1)} fusion(f32[1,128,128]{2,1,0:T(8,128)} %param.28, f32[1,128,128]{2,1,0:T(8,128)} %param.27), kind=kOutput, calls=%fused_computation.12 | convolution fusion | flops 12599296 | bytes 196608 | tf_op jit(solution)/shard_map/dot_general | solution.py:19
  2.9 2.0 %collective-permute-start.1 = (f32[192,128]{1,0:T(8,128)S(1)}, f32[192,128]{1,0:T(8,128)S(1)}, u32[]{:S(2)}, u32[]{:S(2)}) collective-permute-start(f32[192,128]{1,0:T(8,128)S(1)} %pad_maximum_fusion), channel_id=1, source_target_pairs={{32,0},{48,16},{64,32},{80,48},{96,64},{112,80},{128,96},{144,112}... | collective-permute-start | bytes 294920 | tf_op jit(solution)/shard_map/ppermute | solution.py:13
  5.0 1.9 %collective-permute-start = (f32[192,128]{1,0:T(8,128)S(1)}, f32[192,128]{1,0:T(8,128)S(1)}, u32[]{:S(2)}, u32[]{:S(2)}) collective-permute-start(f32[192,128]{1,0:T(8,128)S(1)} %pad_maximum_fusion), channel_id=1, source_target_pairs={{48,0},{64,16},{80,32},{96,48},{112,64},{128,80},{144,96},{160,112... | collective-permute-start | bytes 294920 | tf_op jit(solution)/shard_map/ppermute | solution.py:13
  6.9 7.2 %collective-permute-start.2 = (f32[192,128]{1,0:T(8,128)S(1)}, f32[192,128]{1,0:T(8,128)S(1)}, u32[]{:S(2)}, u32[]{:S(2)}) collective-permute-start(f32[192,128]{1,0:T(8,128)S(1)} %pad_maximum_fusion), channel_id=1, source_target_pairs={{16,0},{32,16},{48,32},{64,48},{80,64},{96,80},{112,96},{128,112},... | collective-permute-start | bytes 294920 | tf_op jit(solution)/shard_map/ppermute | solution.py:13
  14.1 0.7 fusion.44
  14.7 0.2 fusion.19
  15.0 1.3 %collective-permute-done.2 = f32[192,128]{1,0:T(8,128)S(1)} collective-permute-done((f32[192,128]{1,0:T(8,128)S(1)}, f32[192,128]{1,0:T(8,128)S(1)}, u32[]{:S(2)}, u32[]{:S(2)}) %collective-permute-start.2) | collective-permute-done | bytes 98336 | tf_op jit(solution)/shard_map/ppermute | solution.py:13
  16.3 0.2 fusion.17
  16.5 0.2 fusion.46
  16.8 1.9 %collective-permute-start.3 = (f32[192,128]{1,0:T(8,128)S(1)}, f32[192,128]{1,0:T(8,128)S(1)}, u32[]{:S(2)}, u32[]{:S(2)}) collective-permute-start(f32[192,128]{1,0:T(8,128)S(1)} %fusion.41), channel_id=1, source_target_pairs={{64,0},{80,16},{96,32},{112,48},{128,64},{144,80},{160,96},{176,11... | collective-permute-start | bytes 294920 | tf_op jit(solution)/shard_map/ppermute | solution.py:13
  18.7 0.7 compare_and_fusion
  19.4 6.8 %collective-permute-done.3 = f32[192,128]{1,0:T(8,128)S(1)} collective-permute-done((f32[192,128]{1,0:T(8,128)S(1)}, f32[192,128]{1,0:T(8,128)S(1)}, u32[]{:S(2)}, u32[]{:S(2)}) %collective-permute-start.3) | collective-permute-done | bytes 98336 | tf_op jit(solution)/shard_map/ppermute | solution.py:13
  26.2 0.2 convolution_add_fusion.2
  26.4 1.3 %collective-permute-start.4 = (f32[64,128]{1,0:T(8,128)S(1)}, f32[64,128]{1,0:T(8,128)S(1)}, u32[]{:S(2)}, u32[]{:S(2)}) collective-permute-start(f32[64,128]{1,0:T(8,128)S(1)} %convolution_add_fusion.2), channel_id=1, source_target_pairs={{128,0},{144,16},{160,32},{176,48},{192,64},{208,80},{224,96},{240... | collective-permute-start | bytes 98312 | tf_op jit(solution)/shard_map/ppermute | solution.py:13
  27.7 0.2 fusion.15
  27.9 8.4 %collective-permute-done.4 = f32[64,128]{1,0:T(8,128)S(1)} collective-permute-done((f32[64,128]{1,0:T(8,128)S(1)}, f32[64,128]{1,0:T(8,128)S(1)}, u32[]{:S(2)}, u32[]{:S(2)}) %collective-permute-start.4) | collective-permute-done | bytes 32800 | tf_op jit(solution)/shard_map/ppermute | solution.py:13
  36.4 0.2 convolution_add_fusion.1
  36.6 1.3 %collective-permute-start.5 = (f32[64,128]{1,0:T(8,128)S(1)}, f32[64,128]{1,0:T(8,128)S(1)}, u32[]{:S(2)}, u32[]{:S(2)}) collective-permute-start(f32[64,128]{1,0:T(8,128)S(1)} %convolution_add_fusion.1), channel_id=1, source_target_pairs={{128,0},{144,16},{160,32},{176,48},{192,64},{208,80},{224,96},{240... | collective-permute-start | bytes 98312 | tf_op jit(solution)/shard_map/ppermute | solution.py:13
  38.5 7.9 %collective-permute-done.5 = f32[64,128]{1,0:T(8,128)S(1)} collective-permute-done((f32[64,128]{1,0:T(8,128)S(1)}, f32[64,128]{1,0:T(8,128)S(1)}, u32[]{:S(2)}, u32[]{:S(2)}) %collective-permute-start.5) | collective-permute-done | bytes 32800 | tf_op jit(solution)/shard_map/ppermute | solution.py:13
  46.4 0.2 fusion.47
  46.6 1.3 %collective-permute-start.6 = (f32[64,128]{1,0:T(8,128)S(1)}, f32[64,128]{1,0:T(8,128)S(1)}, u32[]{:S(2)}, u32[]{:S(2)}) collective-permute-start(f32[64,128]{1,0:T(8,128)S(1)} %fusion.47), channel_id=1, source_target_pairs={{128,0},{144,16},{160,32},{176,48},{192,64},{208,80},{224,96},{240... | collective-permute-start | bytes 98312 | tf_op jit(solution)/shard_map/ppermute | solution.py:13
  47.9 9.5 %collective-permute-done.6 = f32[64,128]{1,0:T(8,128)S(1)} collective-permute-done((f32[64,128]{1,0:T(8,128)S(1)}, f32[64,128]{1,0:T(8,128)S(1)}, u32[]{:S(2)}, u32[]{:S(2)}) %collective-permute-start.6) | collective-permute-done | bytes 32800 | tf_op jit(solution)/shard_map/ppermute | solution.py:13
  57.3 0.2 convolution_add_fusion
  57.6 0.3 convolution_convert_fusion
  57.9 0.7 gather_fusion
  58.7 0.7 fusion.3
  59.4 1.7 %fusion = f32[32,64,128]{2,0,1:T(8,128)S(1)} fusion(s32[64]{0:T(128)S(1)} %bitcast.89, pred[64]{0:T(512)(128)(4,1)S(1)} %iota_compare_fusion.1, f32[8,8,64,128]{3,2,1,0:T(8,128)S(1)} %bitcast.86), kind=kOutput, calls=%fused_computation.2 | convolution fusion | flops 100667392 | bytes 3146048 | tf_op jit(solution)/shard_map/dot_general | solution.py:81
  61.2 0.6 copy.18
  61.8 21.2 %all_to_all.5 = f32[32,64,128]{2,1,0:T(8,128)S(1)} all-to-all(f32[32,64,128]{2,1,0:T(8,128)S(1)} %copy.18), channel_id=1, replica_groups=mesh['tm'=32,'tile'=16] {'tile'}, dimensions={0} | all-to-all | bytes 2097152 | tf_op jit(solution)/shard_map/all_to_all | solution.py:84
  83.1 0.1 fusion.21
  83.2 0.8 convolution_bitcast_fusion.1
  (28 shorter events, 0.2 us)
Async XLA Ops:
  0.6 58.0 %copy-start = (bf16[1,64,128,128]{3,2,1,0:T(8,128)(2,1)S(1)}, bf16[1,64,128,128]{3,2,1,0:T(8,128)(2,1)}, u32[]{:S(2)}) copy-start(bf16[1,64,128,128]{3,2,1,0:T(8,128)(2,1)} %param.21) | copy-start | bytes 6291460
  0.6 56.9 %copy-start.2 = (bf16[1,8,128,128]{3,2,1,0:T(8,128)(2,1)S(1)}, bf16[1,8,128,128]{3,2,1,0:T(8,128)(2,1)}, u32[]{:S(2)}) copy-start(bf16[1,8,128,128]{3,2,1,0:T(8,128)(2,1)} %param.22) | copy-start | bytes 786436
  0.7 56.9 %copy-start.3 = (bf16[1,8,128,128]{3,2,1,0:T(8,128)(2,1)S(1)}, bf16[1,8,128,128]{3,2,1,0:T(8,128)(2,1)}, u32[]{:S(2)}) copy-start(bf16[1,8,128,128]{3,2,1,0:T(8,128)(2,1)} %param.23) | copy-start | bytes 786436
  0.7 56.9 %copy-start.4 = (bf16[1,8,64,128]{3,2,1,0:T(8,128)(2,1)S(1)}, bf16[1,8,64,128]{3,2,1,0:T(8,128)(2,1)}, u32[]{:S(2)}) copy-start(bf16[1,8,64,128]{3,2,1,0:T(8,128)(2,1)} %param.24) | copy-start | bytes 393220
  2.9 11.8 %collective-permute-start.1 = (f32[192,128]{1,0:T(8,128)S(1)}, f32[192,128]{1,0:T(8,128)S(1)}, u32[]{:S(2)}, u32[]{:S(2)}) collective-permute-start(f32[192,128]{1,0:T(8,128)S(1)} %pad_maximum_fusion), channel_id=1, source_target_pairs={{32,0},{48,16},{64,32},{80,48},{96,64},{112,80},{128,96},{144,112}... | collective-permute-start | bytes 294920 | tf_op jit(solution)/shard_map/ppermute | solution.py:13
  5.0 9.8 %collective-permute-start = (f32[192,128]{1,0:T(8,128)S(1)}, f32[192,128]{1,0:T(8,128)S(1)}, u32[]{:S(2)}, u32[]{:S(2)}) collective-permute-start(f32[192,128]{1,0:T(8,128)S(1)} %pad_maximum_fusion), channel_id=1, source_target_pairs={{48,0},{64,16},{80,32},{96,48},{112,64},{128,80},{144,96},{160,112... | collective-permute-start | bytes 294920 | tf_op jit(solution)/shard_map/ppermute | solution.py:13
  6.9 9.4 %collective-permute-start.2 = (f32[192,128]{1,0:T(8,128)S(1)}, f32[192,128]{1,0:T(8,128)S(1)}, u32[]{:S(2)}, u32[]{:S(2)}) collective-permute-start(f32[192,128]{1,0:T(8,128)S(1)} %pad_maximum_fusion), channel_id=1, source_target_pairs={{16,0},{32,16},{48,32},{64,48},{80,64},{96,80},{112,96},{128,112},... | collective-permute-start | bytes 294920 | tf_op jit(solution)/shard_map/ppermute | solution.py:13
  16.8 9.4 %collective-permute-start.3 = (f32[192,128]{1,0:T(8,128)S(1)}, f32[192,128]{1,0:T(8,128)S(1)}, u32[]{:S(2)}, u32[]{:S(2)}) collective-permute-start(f32[192,128]{1,0:T(8,128)S(1)} %fusion.41), channel_id=1, source_target_pairs={{64,0},{80,16},{96,32},{112,48},{128,64},{144,80},{160,96},{176,11... | collective-permute-start | bytes 294920 | tf_op jit(solution)/shard_map/ppermute | solution.py:13
  26.4 10.0 %collective-permute-start.4 = (f32[64,128]{1,0:T(8,128)S(1)}, f32[64,128]{1,0:T(8,128)S(1)}, u32[]{:S(2)}, u32[]{:S(2)}) collective-permute-start(f32[64,128]{1,0:T(8,128)S(1)} %convolution_add_fusion.2), channel_id=1, source_target_pairs={{128,0},{144,16},{160,32},{176,48},{192,64},{208,80},{224,96},{240... | collective-permute-start | bytes 98312 | tf_op jit(solution)/shard_map/ppermute | solution.py:13
  36.6 9.8 %collective-permute-start.5 = (f32[64,128]{1,0:T(8,128)S(1)}, f32[64,128]{1,0:T(8,128)S(1)}, u32[]{:S(2)}, u32[]{:S(2)}) collective-permute-start(f32[64,128]{1,0:T(8,128)S(1)} %convolution_add_fusion.1), channel_id=1, source_target_pairs={{128,0},{144,16},{160,32},{176,48},{192,64},{208,80},{224,96},{240... | collective-permute-start | bytes 98312 | tf_op jit(solution)/shard_map/ppermute | solution.py:13
  46.6 10.8 %collective-permute-start.6 = (f32[64,128]{1,0:T(8,128)S(1)}, f32[64,128]{1,0:T(8,128)S(1)}, u32[]{:S(2)}, u32[]{:S(2)}) collective-permute-start(f32[64,128]{1,0:T(8,128)S(1)} %fusion.47), channel_id=1, source_target_pairs={{128,0},{144,16},{160,32},{176,48},{192,64},{208,80},{224,96},{240... | collective-permute-start | bytes 98312 | tf_op jit(solution)/shard_map/ppermute | solution.py:13
  57.6 1.9 %copy-start.5 = (f32[64,128]{1,0:T(8,128)}, f32[64,128]{1,0:T(8,128)S(1)}, u32[]{:S(2)}) copy-start(f32[64,128]{1,0:T(8,128)S(1)} %convolution_add_fusion) | copy-start | bytes 98308
  57.9 1.5 %copy-start.1 = (bf16[8,64,128]{2,1,0:T(8,128)(2,1)}, bf16[8,64,128]{2,1,0:T(8,128)(2,1)S(1)}, u32[]{:S(2)}) copy-start(bf16[8,64,128]{2,1,0:T(8,128)(2,1)S(1)} %convolution_convert_fusion) | copy-start | bytes 393220
  58.7 0.8 copy-start.8
  61.8 21.3 %copy-start.7 = (bf16[1,2,64,128]{3,2,1,0:T(8,128)(2,1)S(1)}, bf16[1,2,64,128]{3,2,1,0:T(8,128)(2,1)}, u32[]{:S(2)}) copy-start(bf16[1,2,64,128]{3,2,1,0:T(8,128)(2,1)} %param.26) | copy-start | bytes 98308
  61.8 21.4 %copy-start.6 = (bf16[1,2,128,128]{3,2,1,0:T(8,128)(2,1)S(1)}, bf16[1,2,128,128]{3,2,1,0:T(8,128)(2,1)}, u32[]{:S(2)}) copy-start(bf16[1,2,128,128]{3,2,1,0:T(8,128)(2,1)} %param.25) | copy-start | bytes 196612

commit v5 on v4

--- a/solution.py
+++ b/solution.py
@@ -15,8 +15,8 @@
 
 def chain_multipliers(inverse, nextmat, rhside):
     vectors = rhside.shape[0]
-    b = jnp.dot(rhside, inverse, precision=MID)
-    a = -jnp.dot(nextmat, inverse, precision=MID)
+    b = jnp.dot(rhside, inverse, precision=HIGH)
+    a = -jnp.dot(nextmat, inverse, precision=HIGH)
     size = lax.axis_size("tm")
     by = 1
     if size >= 8:

time: 84.3 us -> 84.4 us (level)
  no operation moved by 1% of the time
where the time goes in v5:
time: 84.4 us; the launch traced here: 84 us
  waiting for transfers between devices  33.1 us (39%)
  blocking collectives  22 us (26%)
  starting transfers between devices  16.9 us (20%)
  matrix products  7.41 us (9%)
  between operations  1.66 us (2%)
  other arithmetic  1.5 us (2%)
  local copies, waits for them, and re-layouts  1.43 us (2%)
    ppermute x7, waiting for transfers between devices, pulled_from(): return lax.ppermute(x, axis, pairs)  33.1 us
    all_to_all x1, blocking collectives, per_device(): spread = lax.all_to_all(whole, 'tile', 0, 0, tiled=True)  22 us
    ppermute x7, starting transfers between devices, pulled_from(): return lax.ppermute(x, axis, pairs)  16.9 us
    dot_general x1, matrix products, per_device(): jnp.dot(placed_in.astype(jnp.float32), products.reshape(slots, -1), preci...  1.71 us
  transfers between devices with their start and end apart: 7, of which 5 were waited for; matrix products, arithmetic and copies ran while one was open for 2% of the time, Pallas kernels for 0%

profile of v5, /device:TPU:96, one launch (start us, length us, event | category | flops | bytes accessed | tf_op | source)
XLA Modules:
  0.0 84.0 jit_solution(1415504571141604721)
XLA Ops:
  0.7 1.2 %fusion.25 = f32[64,128]{1,0:T(8,128)S(1)} fusion(f32[1,128,128]{2,1,0:T(8,128)} %param.27, f32[1,64,128]{2,1,0:T(8,128)} %param.29), kind=kOutput, calls=%fused_computation.35 | convolution fusion | flops 12582912 | bytes 131072 | tf_op jit(solution)/shard_map/dot_general | solution.py:18
  1.9 1.1 %convolution_negate_fusion = f32[128,128]{1,0:T(8,128)S(1)} fusion(f32[1,128,128]{2,1,0:T(8,128)} %param.28, f32[1,128,128]{2,1,0:T(8,128)} %param.27), kind=kOutput, calls=%fused_computation.12 | convolution fusion | flops 25182208 | bytes 196608 | tf_op jit(solution)/shard_map/dot_general | solution.py:19
  3.0 2.0 %collective-permute-start.1 = (f32[192,128]{1,0:T(8,128)S(1)}, f32[192,128]{1,0:T(8,128)S(1)}, u32[]{:S(2)}, u32[]{:S(2)}) collective-permute-start(f32[192,128]{1,0:T(8,128)S(1)} %pad_maximum_fusion), channel_id=1, source_target_pairs={{32,0},{48,16},{64,32},{80,48},{96,64},{112,80},{128,96},{144,112}... | collective-permute-start | bytes 294920 | tf_op jit(solution)/shard_map/ppermute | solution.py:13
  5.0 1.9 %collective-permute-start = (f32[192,128]{1,0:T(8,128)S(1)}, f32[192,128]{1,0:T(8,128)S(1)}, u32[]{:S(2)}, u32[]{:S(2)}) collective-permute-start(f32[192,128]{1,0:T(8,128)S(1)} %pad_maximum_fusion), channel_id=1, source_target_pairs={{48,0},{64,16},{80,32},{96,48},{112,64},{128,80},{144,96},{160,112... | collective-permute-start | bytes 294920 | tf_op jit(solution)/shard_map/ppermute | solution.py:13
  6.9 7.2 %collective-permute-start.2 = (f32[192,128]{1,0:T(8,128)S(1)}, f32[192,128]{1,0:T(8,128)S(1)}, u32[]{:S(2)}, u32[]{:S(2)}) collective-permute-start(f32[192,128]{1,0:T(8,128)S(1)} %pad_maximum_fusion), channel_id=1, source_target_pairs={{16,0},{32,16},{48,32},{64,48},{80,64},{96,80},{112,96},{128,112},... | collective-permute-start | bytes 294920 | tf_op jit(solution)/shard_map/ppermute | solution.py:13
  14.1 0.7 fusion.44
  14.8 0.2 fusion.19
  15.0 1.3 %collective-permute-done.2 = f32[192,128]{1,0:T(8,128)S(1)} collective-permute-done((f32[192,128]{1,0:T(8,128)S(1)}, f32[192,128]{1,0:T(8,128)S(1)}, u32[]{:S(2)}, u32[]{:S(2)}) %collective-permute-start.2) | collective-permute-done | bytes 98336 | tf_op jit(solution)/shard_map/ppermute | solution.py:13
  16.3 0.2 fusion.17
  16.6 0.2 fusion.46
  16.8 1.9 %collective-permute-start.3 = (f32[192,128]{1,0:T(8,128)S(1)}, f32[192,128]{1,0:T(8,128)S(1)}, u32[]{:S(2)}, u32[]{:S(2)}) collective-permute-start(f32[192,128]{1,0:T(8,128)S(1)} %fusion.41), channel_id=1, source_target_pairs={{64,0},{80,16},{96,32},{112,48},{128,64},{144,80},{160,96},{176,11... | collective-permute-start | bytes 294920 | tf_op jit(solution)/shard_map/ppermute | solution.py:13
  18.8 0.7 compare_and_fusion
  19.4 6.9 %collective-permute-done.3 = f32[192,128]{1,0:T(8,128)S(1)} collective-permute-done((f32[192,128]{1,0:T(8,128)S(1)}, f32[192,128]{1,0:T(8,128)S(1)}, u32[]{:S(2)}, u32[]{:S(2)}) %collective-permute-start.3) | collective-permute-done | bytes 98336 | tf_op jit(solution)/shard_map/ppermute | solution.py:13
  26.3 0.2 convolution_add_fusion.2
  26.5 1.3 %collective-permute-start.4 = (f32[64,128]{1,0:T(8,128)S(1)}, f32[64,128]{1,0:T(8,128)S(1)}, u32[]{:S(2)}, u32[]{:S(2)}) collective-permute-start(f32[64,128]{1,0:T(8,128)S(1)} %convolution_add_fusion.2), channel_id=1, source_target_pairs={{128,0},{144,16},{160,32},{176,48},{192,64},{208,80},{224,96},{240... | collective-permute-start | bytes 98312 | tf_op jit(solution)/shard_map/ppermute | solution.py:13
  27.8 0.2 fusion.15
  28.0 8.4 %collective-permute-done.4 = f32[64,128]{1,0:T(8,128)S(1)} collective-permute-done((f32[64,128]{1,0:T(8,128)S(1)}, f32[64,128]{1,0:T(8,128)S(1)}, u32[]{:S(2)}, u32[]{:S(2)}) %collective-permute-start.4) | collective-permute-done | bytes 32800 | tf_op jit(solution)/shard_map/ppermute | solution.py:13
  36.4 0.2 convolution_add_fusion.1
  36.6 1.3 %collective-permute-start.5 = (f32[64,128]{1,0:T(8,128)S(1)}, f32[64,128]{1,0:T(8,128)S(1)}, u32[]{:S(2)}, u32[]{:S(2)}) collective-permute-start(f32[64,128]{1,0:T(8,128)S(1)} %convolution_add_fusion.1), channel_id=1, source_target_pairs={{128,0},{144,16},{160,32},{176,48},{192,64},{208,80},{224,96},{240... | collective-permute-start | bytes 98312 | tf_op jit(solution)/shard_map/ppermute | solution.py:13
  38.6 7.8 %collective-permute-done.5 = f32[64,128]{1,0:T(8,128)S(1)} collective-permute-done((f32[64,128]{1,0:T(8,128)S(1)}, f32[64,128]{1,0:T(8,128)S(1)}, u32[]{:S(2)}, u32[]{:S(2)}) %collective-permute-start.5) | collective-permute-done | bytes 32800 | tf_op jit(solution)/shard_map/ppermute | solution.py:13
  46.4 0.2 fusion.47
  46.6 1.3 %collective-permute-start.6 = (f32[64,128]{1,0:T(8,128)S(1)}, f32[64,128]{1,0:T(8,128)S(1)}, u32[]{:S(2)}, u32[]{:S(2)}) collective-permute-start(f32[64,128]{1,0:T(8,128)S(1)} %fusion.47), channel_id=1, source_target_pairs={{128,0},{144,16},{160,32},{176,48},{192,64},{208,80},{224,96},{240... | collective-permute-start | bytes 98312 | tf_op jit(solution)/shard_map/ppermute | solution.py:13
  47.9 8.7 %collective-permute-done.6 = f32[64,128]{1,0:T(8,128)S(1)} collective-permute-done((f32[64,128]{1,0:T(8,128)S(1)}, f32[64,128]{1,0:T(8,128)S(1)}, u32[]{:S(2)}, u32[]{:S(2)}) %collective-permute-start.6) | collective-permute-done | bytes 32800 | tf_op jit(solution)/shard_map/ppermute | solution.py:13
  56.6 0.2 convolution_add_fusion
  56.8 0.3 convolution_convert_fusion
  57.2 0.7 gather_fusion
  57.9 0.7 fusion.3
  58.7 1.7 %fusion = f32[32,64,128]{2,0,1:T(8,128)S(1)} fusion(s32[64]{0:T(128)S(1)} %bitcast.89, pred[64]{0:T(512)(128)(4,1)S(1)} %iota_compare_fusion.1, f32[8,8,64,128]{3,2,1,0:T(8,128)S(1)} %bitcast.86), kind=kOutput, calls=%fused_computation.2 | convolution fusion | flops 100667392 | bytes 3146048 | tf_op jit(solution)/shard_map/dot_general | solution.py:81
  60.4 0.6 copy.18
  61.0 22.0 %all_to_all.5 = f32[32,64,128]{2,1,0:T(8,128)S(1)} all-to-all(f32[32,64,128]{2,1,0:T(8,128)S(1)} %copy.18), channel_id=1, replica_groups=mesh['tm'=32,'tile'=16] {'tile'}, dimensions={0} | all-to-all | bytes 2097152 | tf_op jit(solution)/shard_map/all_to_all | solution.py:84
  83.1 0.1 fusion.21
  83.2 0.8 convolution_bitcast_fusion.1
  (28 shorter events, 0.2 us)
Async XLA Ops:
  0.6 57.3 %copy-start = (bf16[1,64,128,128]{3,2,1,0:T(8,128)(2,1)S(1)}, bf16[1,64,128,128]{3,2,1,0:T(8,128)(2,1)}, u32[]{:S(2)}) copy-start(bf16[1,64,128,128]{3,2,1,0:T(8,128)(2,1)} %param.21) | copy-start | bytes 6291460
  0.6 56.1 %copy-start.2 = (bf16[1,8,128,128]{3,2,1,0:T(8,128)(2,1)S(1)}, bf16[1,8,128,128]{3,2,1,0:T(8,128)(2,1)}, u32[]{:S(2)}) copy-start(bf16[1,8,128,128]{3,2,1,0:T(8,128)(2,1)} %param.22) | copy-start | bytes 786436
  0.7 56.1 %copy-start.3 = (bf16[1,8,128,128]{3,2,1,0:T(8,128)(2,1)S(1)}, bf16[1,8,128,128]{3,2,1,0:T(8,128)(2,1)}, u32[]{:S(2)}) copy-start(bf16[1,8,128,128]{3,2,1,0:T(8,128)(2,1)} %param.23) | copy-start | bytes 786436
  0.7 56.1 %copy-start.4 = (bf16[1,8,64,128]{3,2,1,0:T(8,128)(2,1)S(1)}, bf16[1,8,64,128]{3,2,1,0:T(8,128)(2,1)}, u32[]{:S(2)}) copy-start(bf16[1,8,64,128]{3,2,1,0:T(8,128)(2,1)} %param.24) | copy-start | bytes 393220
  3.0 11.8 %collective-permute-start.1 = (f32[192,128]{1,0:T(8,128)S(1)}, f32[192,128]{1,0:T(8,128)S(1)}, u32[]{:S(2)}, u32[]{:S(2)}) collective-permute-start(f32[192,128]{1,0:T(8,128)S(1)} %pad_maximum_fusion), channel_id=1, source_target_pairs={{32,0},{48,16},{64,32},{80,48},{96,64},{112,80},{128,96},{144,112}... | collective-permute-start | bytes 294920 | tf_op jit(solution)/shard_map/ppermute | solution.py:13
  5.0 9.8 %collective-permute-start = (f32[192,128]{1,0:T(8,128)S(1)}, f32[192,128]{1,0:T(8,128)S(1)}, u32[]{:S(2)}, u32[]{:S(2)}) collective-permute-start(f32[192,128]{1,0:T(8,128)S(1)} %pad_maximum_fusion), channel_id=1, source_target_pairs={{48,0},{64,16},{80,32},{96,48},{112,64},{128,80},{144,96},{160,112... | collective-permute-start | bytes 294920 | tf_op jit(solution)/shard_map/ppermute | solution.py:13
  6.9 9.4 %collective-permute-start.2 = (f32[192,128]{1,0:T(8,128)S(1)}, f32[192,128]{1,0:T(8,128)S(1)}, u32[]{:S(2)}, u32[]{:S(2)}) collective-permute-start(f32[192,128]{1,0:T(8,128)S(1)} %pad_maximum_fusion), channel_id=1, source_target_pairs={{16,0},{32,16},{48,32},{64,48},{80,64},{96,80},{112,96},{128,112},... | collective-permute-start | bytes 294920 | tf_op jit(solution)/shard_map/ppermute | solution.py:13
  16.8 9.4 %collective-permute-start.3 = (f32[192,128]{1,0:T(8,128)S(1)}, f32[192,128]{1,0:T(8,128)S(1)}, u32[]{:S(2)}, u32[]{:S(2)}) collective-permute-start(f32[192,128]{1,0:T(8,128)S(1)} %fusion.41), channel_id=1, source_target_pairs={{64,0},{80,16},{96,32},{112,48},{128,64},{144,80},{160,96},{176,11... | collective-permute-start | bytes 294920 | tf_op jit(solution)/shard_map/ppermute | solution.py:13
  26.5 10.0 %collective-permute-start.4 = (f32[64,128]{1,0:T(8,128)S(1)}, f32[64,128]{1,0:T(8,128)S(1)}, u32[]{:S(2)}, u32[]{:S(2)}) collective-permute-start(f32[64,128]{1,0:T(8,128)S(1)} %convolution_add_fusion.2), channel_id=1, source_target_pairs={{128,0},{144,16},{160,32},{176,48},{192,64},{208,80},{224,96},{240... | collective-permute-start | bytes 98312 | tf_op jit(solution)/shard_map/ppermute | solution.py:13
  36.6 9.8 %collective-permute-start.5 = (f32[64,128]{1,0:T(8,128)S(1)}, f32[64,128]{1,0:T(8,128)S(1)}, u32[]{:S(2)}, u32[]{:S(2)}) collective-permute-start(f32[64,128]{1,0:T(8,128)S(1)} %convolution_add_fusion.1), channel_id=1, source_target_pairs={{128,0},{144,16},{160,32},{176,48},{192,64},{208,80},{224,96},{240... | collective-permute-start | bytes 98312 | tf_op jit(solution)/shard_map/ppermute | solution.py:13
  46.6 10.0 %collective-permute-start.6 = (f32[64,128]{1,0:T(8,128)S(1)}, f32[64,128]{1,0:T(8,128)S(1)}, u32[]{:S(2)}, u32[]{:S(2)}) collective-permute-start(f32[64,128]{1,0:T(8,128)S(1)} %fusion.47), channel_id=1, source_target_pairs={{128,0},{144,16},{160,32},{176,48},{192,64},{208,80},{224,96},{240... | collective-permute-start | bytes 98312 | tf_op jit(solution)/shard_map/ppermute | solution.py:13
  56.8 1.9 %copy-start.5 = (f32[64,128]{1,0:T(8,128)}, f32[64,128]{1,0:T(8,128)S(1)}, u32[]{:S(2)}) copy-start(f32[64,128]{1,0:T(8,128)S(1)} %convolution_add_fusion) | copy-start | bytes 98308
  57.1 1.5 %copy-start.1 = (bf16[8,64,128]{2,1,0:T(8,128)(2,1)}, bf16[8,64,128]{2,1,0:T(8,128)(2,1)S(1)}, u32[]{:S(2)}) copy-start(bf16[8,64,128]{2,1,0:T(8,128)(2,1)S(1)} %convolution_convert_fusion) | copy-start | bytes 393220
  57.9 0.8 copy-start.8
  61.0 22.1 %copy-start.7 = (bf16[1,2,64,128]{3,2,1,0:T(8,128)(2,1)S(1)}, bf16[1,2,64,128]{3,2,1,0:T(8,128)(2,1)}, u32[]{:S(2)}) copy-start(bf16[1,2,64,128]{3,2,1,0:T(8,128)(2,1)} %param.26) | copy-start | bytes 98308
  61.0 22.2 %copy-start.6 = (bf16[1,2,128,128]{3,2,1,0:T(8,128)(2,1)S(1)}, bf16[1,2,128,128]{3,2,1,0:T(8,128)(2,1)}, u32[]{:S(2)}) copy-start(bf16[1,2,128,128]{3,2,1,0:T(8,128)(2,1)} %param.25) | copy-start | bytes 196612
